TPU v7x, 128 devices: a whole 4x4x4 slice. The times are simulated.
128 devices in a mesh: row: 8 (over y, core), col: 16 (over z, x).
Axes of the slice: x: 4, y: 4, z: 4, core: 2. Of those that a mesh axis runs over, the one named last changes fastest.
Arguments:
- forward_head: bfloat16 [4, 2048, 1000], P(None, 'col'), may hold values from -6 to 6
- forward_tail: bfloat16 [57344, 1000], P(('col', 'row')), may hold values from -6 to 6
- forward_inverse: bfloat16 [4, 2048, 2048], P(None, 'col', 'row'), may hold values from -1.5 to 1.5, as said below
- forward_coupling: bfloat16 [6, 2048, 2048], P(None, 'row', 'col'), may hold values from -0.078125 to 0.078125
- forward_slab: bfloat16 [4, 2048, 57344], P(None, 'row', 'col'), may hold values from -0.0625 to 0.0625
- backward_head: bfloat16 [4, 2048, 1000], P(None, 'row'), may hold values from -6 to 6
- backward_tail: bfloat16 [57344, 1000], P(('row', 'col')), may hold values from -6 to 6
- backward_inverse: bfloat16 [4, 2048, 2048], P(None, 'col', 'row'), may hold values from -1.5 to 1.5, as said below
- backward_coupling: bfloat16 [6, 2048, 2048], P(None, 'row', 'col'), may hold values from -0.078125 to 0.078125
- backward_slab: bfloat16 [57344, 4, 2048], P('row', None, 'col'), may hold values from -0.0625 to 0.0625
Outputs:
- lower_head: bfloat16 [4, 2048, 1000], P(None, 'row')
- lower_tail: bfloat16 [57344, 1000], P(('col', 'row'))
- upper_head: bfloat16 [4, 2048, 1000], P(None, 'col')
- upper_tail: bfloat16 [57344, 1000], P(('row', 'col'))
Inputs may be any that keep to these rules, and one draw needn't show every extreme that they name: Each block of forward_inverse is upper triangular with diagonal entries of magnitude 0.5 to 1.5. Each block of backward_inverse is upper triangular with diagonal entries of magnitude 0.5 to 1.5.
All inputs are finite; a program needn't handle non-finite values.
Results may differ from a plain program's by a relative error of at most 0.03.
Values may be sent and summed in bfloat16 or wider, within the bound.
No kernel may reach another device: no remote copies, remote signals or barrier semaphores. Data moves between devices by JAX's collectives and lax.ppermute only.
A program may use at most 192 MiB of HBM per device.

v0:
```python
import jax
import jax.numpy as jnp
from jax import lax
from jax.experimental.layout import Layout, with_layout_constraint
from jax.sharding import PartitionSpec as P

ROW_INNER = 2
COL_INNER = 4


def shift_pairs(n, inner, sub, d):
    outer = n // inner
    pairs = []
    for o in range(outer):
        for i in range(inner):
            if sub == "inner":
                pairs.append((o * inner + i, o * inner + (i + d) % inner))
            else:
                pairs.append((o * inner + i, ((o + d) % outer) * inner + i))
    return pairs


def sub_index(axis, inner, sub):
    a = lax.axis_index(axis)
    return a % inner if sub == "inner" else a // inner


def sub_size(n, inner, sub):
    return inner if sub == "inner" else n // inner


def ar_direct(v, axis, n, inner, sub):
    size = sub_size(n, inner, sub)
    acc = v.astype(jnp.float32)
    send = v.astype(jnp.bfloat16)
    for d in range(1, size):
        acc = acc + lax.ppermute(send, axis, shift_pairs(n, inner, sub, d)).astype(jnp.float32)
    return acc


def rs_direct(v, axis, n, inner, sub):
    size = sub_size(n, inner, sub)
    me = sub_index(axis, inner, sub)
    pieces = v.reshape(size, v.shape[0] // size, v.shape[1])
    acc = lax.dynamic_index_in_dim(pieces, me, 0, keepdims=False).astype(jnp.float32)
    for d in range(1, size):
        sel = lax.dynamic_index_in_dim(pieces, (me + d) % size, 0, keepdims=False)
        acc = acc + lax.ppermute(
            sel.astype(jnp.bfloat16), axis, shift_pairs(n, inner, sub, d)
        ).astype(jnp.float32)
    return acc


def ag_direct(p, axis, n, inner, sub):
    size = sub_size(n, inner, sub)
    me = sub_index(axis, inner, sub)
    got = [p] + [lax.ppermute(p, axis, shift_pairs(n, inner, sub, -d)) for d in range(1, size)]
    stacked = jnp.roll(jnp.stack(got), me, axis=0)
    return stacked.reshape(size * p.shape[0], p.shape[1])


def rs_hier(value, axis, inner):
    n = lax.axis_size(axis)
    outer = n // inner
    rows = value.shape[0] // n
    me_in = sub_index(axis, inner, "inner")
    me_out = sub_index(axis, inner, "outer")
    grid = value.reshape(outer, inner, rows, value.shape[1])
    received = None
    for d in range(1, inner):
        sel = lax.dynamic_index_in_dim(grid, (me_in + d) % inner, 1, keepdims=False)
        got = lax.ppermute(sel, axis, shift_pairs(n, inner, "inner", d)).astype(jnp.float32)
        received = got if received is None else received + got
    acc = lax.dynamic_index_in_dim(grid, me_in, 1, keepdims=False).astype(jnp.float32) + received
    half = acc.astype(jnp.bfloat16)
    total = lax.dynamic_index_in_dim(
        lax.dynamic_index_in_dim(grid, me_in, 1, keepdims=False), me_out, 0, keepdims=False
    ).astype(jnp.float32) + lax.dynamic_index_in_dim(received, me_out, 0, keepdims=False)
    for d in range(1, outer):
        sel = lax.dynamic_index_in_dim(half, (me_out + d) % outer, 0, keepdims=False)
        total = total + lax.ppermute(sel, axis, shift_pairs(n, inner, "outer", d)).astype(jnp.float32)
    return total


def allreduce(value, axis, inner, hold=None):
    n = lax.axis_size(axis)
    piece = rs_direct(value.astype(jnp.bfloat16), axis, n, inner, "inner")
    piece = ar_direct(piece.astype(jnp.bfloat16), axis, n, inner, "outer").astype(jnp.bfloat16)
    if hold is not None:
        piece, _ = lax.optimization_barrier((piece, hold))
    return ag_direct(piece, axis, n, inner, "inner")


def reduce_row(value):
    return allreduce(value, "row", ROW_INNER)


def reduce_col(value, hold=None):
    return allreduce(value, "col", COL_INNER, hold)


def leading_dot(left, right):
    return lax.dot_general(
        left, right, (((0,), (0,)), ((), ())), preferred_element_type=jnp.float32
    )


def local(
    forward_head,
    forward_tail,
    forward_inverse,
    forward_coupling,
    forward_slab,
    backward_head,
    backward_tail,
    backward_inverse,
    backward_coupling,
    backward_slab,
):
    classes = forward_head.shape[2]
    panels = forward_head.shape[0]
    upper_list = [None] * panels
    lower_list = []
    for step in range(panels):
        panel_index = panels - 1 - step
        if panel_index == panels - 1:
            shifted = backward_head[panel_index]
        else:
            summed = None
            for later_panel in range(panel_index + 1, panels):
                block = backward_coupling[later_panel * (later_panel - 1) // 2 + panel_index]
                product = jnp.dot(
                    block, upper_list[later_panel], preferred_element_type=jnp.float32
                )
                summed = product if summed is None else summed + product
            pulled = reduce_col(summed).astype(jnp.float32)
            shifted = (backward_head[panel_index].astype(jnp.float32) - pulled).astype(jnp.bfloat16)
        upper_list[panel_index] = reduce_row(
            jnp.dot(backward_inverse[panel_index], shifted, preferred_element_type=jnp.float32)
        )

        panel_index = step
        if panel_index == 0:
            adjusted = forward_head[0]
        else:
            summed = leading_dot(
                forward_coupling[panel_index * (panel_index - 1) // 2], lower_list[0]
            )
            for earlier in range(1, panel_index):
                summed = summed + leading_dot(
                    forward_coupling[panel_index * (panel_index - 1) // 2 + earlier],
                    lower_list[earlier],
                )
            coupling = reduce_row(summed).astype(jnp.float32)
            adjusted = (forward_head[panel_index].astype(jnp.float32) - coupling).astype(
                jnp.bfloat16
            )
        lead = shifted
        if step == panels - 1:
            upper_head = jnp.stack(upper_list)
            panel_cols = upper_head.shape[1]
            flat_back = backward_slab.reshape(backward_slab.shape[0], panels * panel_cols)
            flat_upper = upper_head.reshape(panels * panel_cols, classes)
            upper_partial = with_layout_constraint(
                jnp.dot(flat_back, flat_upper, preferred_element_type=jnp.float32).astype(
                    jnp.bfloat16
                ),
                Layout(major_to_minor=(0, 1)),
            )
        partial, _ = lax.optimization_barrier(
            (leading_dot(forward_inverse[panel_index], adjusted), lead)
        )
        lower_list.append(reduce_col(partial, upper_partial if step == panels - 1 else None))
    lower_head = jnp.stack(lower_list)
    panel_rows = lower_head.shape[1]
    early = panels - 1
    early_slab = forward_slab[:early].reshape(early * panel_rows, forward_slab.shape[2])
    split = 512 if classes > 512 else classes
    updates = []
    for lo, hi in ((0, split), (split, classes)):
        if hi <= lo:
            continue
        part = lower_head[:, :, lo:hi]
        early_partial = with_layout_constraint(
            leading_dot(early_slab, part[:early].reshape(early * panel_rows, hi - lo)),
            Layout(major_to_minor=(0, 1)),
        )
        lower_partial = with_layout_constraint(
            (early_partial + leading_dot(forward_slab[early], part[early])).astype(jnp.bfloat16),
            Layout(major_to_minor=(0, 1)),
        )
        updates.append(rs_hier(lower_partial, "row", ROW_INNER))
    lower_update = jnp.concatenate(updates, axis=1)
    lower_tail = (forward_tail.astype(jnp.float32) - lower_update).astype(jnp.bfloat16)
    upper_update = lax.psum_scatter(
        upper_partial,
        "col",
        scatter_dimension=0,
        tiled=True,
    ).astype(jnp.float32)
    upper_tail = (backward_tail.astype(jnp.float32) - upper_update).astype(jnp.bfloat16)
    return (lower_head, lower_tail, upper_head, upper_tail)


def solution(mesh):
    in_specs = (
        P(None, "col", None),
        P(("col", "row"), None),
        P(None, "col", "row"),
        P(None, "row", "col"),
        P(None, "row", "col"),
        P(None, "row", None),
        P(("row", "col"), None),
        P(None, "col", "row"),
        P(None, "row", "col"),
        P("row", None, "col"),
    )
    out_specs = (
        P(None, "row", None),
        P(("col", "row"), None),
        P(None, "col", None),
        P(("row", "col"), None),
    )
    return jax.shard_map(local, mesh=mesh, in_specs=in_specs, out_specs=out_specs, check_vma=False)
```

profile of v0, /device:TPU:1, one launch (start us, length us, event | category | flops | bytes accessed | tf_op | source)
XLA Modules:
  0.0 385.3 jit_solution(14743241242509214363)
XLA Ops:
  22.1 2.8 collective-permute-start.51
  27.1 3.8 collective-permute-start.5
  49.4 4.2 %collective-permute-start.9 = (bf16[64,1000]{1,0:T(8,128)(2,1)S(1)}, bf16[64,1000]{1,0:T(8,128)(2,1)S(1)}, u32[]{:S(2)}, u32[]{:S(2)}) collective-permute-start(bf16[64,1000]{1,0:T(8,128)(2,1)S(1)} %dynamic-slice_bitcast_fusion.32), channel_id=1, source_target_pairs={{0,16},{16,0},{32,48},{48,32},{64,80},{80,64},{96,112},{112,96},{1... | collective-permute-start | bytes 384008 | tf_op jit(solution)/shard_map/ppermute | solution.py:48
  57.4 2.8 collective-permute-start.12
  65.5 3.6 collective-permute-start.60
  94.2 3.6 collective-permute-done.63
  101.3 2.9 collective-permute-start.21
  115.4 9.7 %collective-permute-start.72 = (bf16[64,1000]{1,0:T(8,128)(2,1)S(1)}, bf16[64,1000]{1,0:T(8,128)(2,1)S(1)}, u32[]{:S(2)}, u32[]{:S(2)}) collective-permute-start(bf16[64,1000]{1,0:T(8,128)(2,1)S(1)} %fusion.130), channel_id=1, source_target_pairs={{0,12},{1,13},{2,14},{3,15},{4,0},{5,1},{6,2},{7,3},{8,4},{9,5},{1... | collective-permute-start | bytes 384008 | tf_op jit(solution)/shard_map/ppermute | solution.py:37
  127.2 4.5 %collective-permute-start.23 = (bf16[64,1000]{1,0:T(8,128)(2,1)S(1)}, bf16[64,1000]{1,0:T(8,128)(2,1)S(1)}, u32[]{:S(2)}, u32[]{:S(2)}) collective-permute-start(bf16[64,1000]{1,0:T(8,128)(2,1)S(1)} %dynamic-slice_bitcast_fusion.28), channel_id=1, source_target_pairs={{0,16},{16,0},{32,48},{48,32},{64,80},{80,64},{96,112},{112,96},{1... | collective-permute-start | bytes 384008 | tf_op jit(solution)/shard_map/ppermute | solution.py:48
  142.1 6.2 %collective-permute-start.76 = (bf16[64,1000]{1,0:T(8,128)(2,1)S(1)}, bf16[64,1000]{1,0:T(8,128)(2,1)S(1)}, u32[]{:S(2)}, u32[]{:S(2)}) collective-permute-start(bf16[64,1000]{1,0:T(8,128)(2,1)S(1)} %dynamic-slice_bitcast_fusion.12), channel_id=1, source_target_pairs={{0,16},{16,0},{32,48},{48,32},{64,80},{80,64},{96,112},{112,96},{1... | collective-permute-start | bytes 384008 | tf_op jit(solution)/shard_map/ppermute | solution.py:48
  148.4 3.0 collective-permute-start.27
  158.5 3.4 collective-permute-done.77
  182.9 3.5 collective-permute-start.36
  197.3 3.6 collective-permute-done.88
  204.7 3.5 collective-permute-start.90
  210.8 3.3 collective-permute-done.93
  215.4 3.8 collective-permute-done.91
  222.8 14.1 %fusion = bf16[7168,1000]{1,0:T(8,128)(2,1)} fusion(bf16[4,128,1000]{1,2,0:T(8,128)(2,1)S(1)} %pad_maximum_fusion.2, bf16[7168,4,128]{2,1,0:T(4,128)(2,1)} %param.23), kind=kOutput, calls=%fused_computation.1 | convolution fusion | flops 7347200000 | bytes 22700032 | tf_op jit(solution)/shard_map/dot_general | solution.py:165
  242.2 3.4 collective-permute-done.40
  247.4 3.9 %collective-permute-done.38 = bf16[64,1000]{1,0:T(8,128)(2,1)S(1)} collective-permute-done((bf16[64,1000]{1,0:T(8,128)(2,1)S(1)}, bf16[64,1000]{1,0:T(8,128)(2,1)S(1)}, u32[]{:S(2)}, u32[]{:S(2)}) %collective-permute-start.38) | collective-permute-done | bytes 128032 | tf_op jit(solution)/shard_map/ppermute | solution.py:37
  258.1 5.7 %collective-permute-done.42 = bf16[64,1000]{1,0:T(8,128)(2,1)S(1)} collective-permute-done((bf16[64,1000]{1,0:T(8,128)(2,1)S(1)}, bf16[64,1000]{1,0:T(8,128)(2,1)S(1)}, u32[]{:S(2)}, u32[]{:S(2)}) %collective-permute-start.42) | collective-permute-done | bytes 128032 | tf_op jit(solution)/shard_map/ppermute | solution.py:48
  263.8 6.3 %collective-permute-done.43 = bf16[64,1000]{1,0:T(8,128)(2,1)S(1)} collective-permute-done((bf16[64,1000]{1,0:T(8,128)(2,1)S(1)}, bf16[64,1000]{1,0:T(8,128)(2,1)S(1)}, u32[]{:S(2)}, u32[]{:S(2)}) %collective-permute-start.43) | collective-permute-done | bytes 128032 | tf_op jit(solution)/shard_map/ppermute | solution.py:48
  271.9 5.7 %collective-permute-done.47 = bf16[64,1000]{1,0:T(8,128)(2,1)S(1)} collective-permute-done((bf16[64,1000]{1,0:T(8,128)(2,1)S(1)}, bf16[64,1000]{1,0:T(8,128)(2,1)S(1)}, u32[]{:S(2)}, u32[]{:S(2)}) %collective-permute-start.47) | collective-permute-done | bytes 128032 | tf_op jit(solution)/shard_map/ppermute | solution.py:37
  279.2 3.9 %collective-permute-done.45 = bf16[64,1000]{1,0:T(8,128)(2,1)S(1)} collective-permute-done((bf16[64,1000]{1,0:T(8,128)(2,1)S(1)}, bf16[64,1000]{1,0:T(8,128)(2,1)S(1)}, u32[]{:S(2)}, u32[]{:S(2)}) %collective-permute-start.45) | collective-permute-done | bytes 128032 | tf_op jit(solution)/shard_map/ppermute | solution.py:37
  287.2 4.3 %collective-permute-done.97 = bf16[64,1000]{1,0:T(8,128)(2,1)S(1)} collective-permute-done((bf16[64,1000]{1,0:T(8,128)(2,1)S(1)}, bf16[64,1000]{1,0:T(8,128)(2,1)S(1)}, u32[]{:S(2)}, u32[]{:S(2)}) %collective-permute-start.97) | collective-permute-done | bytes 128032 | tf_op jit(solution)/shard_map/ppermute | solution.py:57
  291.5 5.0 %collective-permute-done.96 = bf16[64,1000]{1,0:T(8,128)(2,1)S(1)} collective-permute-done((bf16[64,1000]{1,0:T(8,128)(2,1)S(1)}, bf16[64,1000]{1,0:T(8,128)(2,1)S(1)}, u32[]{:S(2)}, u32[]{:S(2)}) %collective-permute-start.96) | collective-permute-done | bytes 128032 | tf_op jit(solution)/shard_map/ppermute | solution.py:57
  298.7 2.9 fusion.8
  301.7 7.5 %fusion.1 = bf16[3584,488]{1,0:T(8,128)(2,1)S(1)} fusion(f32[488,3584]{0,1:T(8,128)S(1)} %fusion.8, bf16[4,256,3584]{2,1,0:T(8,128)(2,1)} %param.18, bf16[3,256,1000]{2,1,0:T(8,128)(2,1)S(1)} %pad_maximum_fusion.1), kind=kOutput, calls=%fused_computation.3 | convolution fusion | flops 2689949696 | bytes 17129472 | tf_op jit(solution)/shard_map/dot_general | solution.py:103
  310.7 2.9 collective-permute-start.102
  316.2 6.0 %fusion.2 = bf16[3584,512]{1,0:T(8,128)(2,1)S(1)} fusion(f32[512,3584]{0,1:T(8,128)S(1)} %fusion.10, bf16[4,256,3584]{2,1,0:T(8,128)(2,1)} %param.18, bf16[3,256,1000]{2,1,0:T(8,128)(2,1)S(1)} %pad_maximum_fusion.1), kind=kOutput, calls=%fused_computation.5 | convolution fusion | flops 2822242304 | bytes 19136512 | tf_op jit(solution)/shard_map/dot_general | solution.py:103
  338.4 14.6 %collective-permute-done.103 = bf16[448,488]{1,0:T(8,128)(2,1)S(1)} collective-permute-done((bf16[448,488]{1,0:T(8,128)(2,1)S(1)}, bf16[448,488]{1,0:T(8,128)(2,1)S(1)}, u32[]{:S(2)}, u32[]{:S(2)}) %collective-permute-start.103) | collective-permute-done | bytes 437280 | tf_op jit(solution)/shard_map/ppermute | solution.py:81
  362.6 10.2 %collective-permute-done.99 = bf16[448,512]{1,0:T(8,128)(2,1)} collective-permute-done((bf16[448,512]{1,0:T(8,128)(2,1)}, bf16[448,512]{1,0:T(8,128)(2,1)}, u32[]{:S(2)}, u32[]{:S(2)}) %collective-permute-start.99) | collective-permute-done | bytes 458784 | tf_op jit(solution)/shard_map/ppermute | solution.py:81
  (347 shorter events, 205.3 us)
Async XLA Ops:
  7.2 368.7 %reduce-scatter.2.cloned.1.call-start = ((), (), s32[]{:S(2)}) async-start(), calls=%async_computation.1 | async-start | bytes 15597568 | tf_op jit(solution)/shard_map/reduce_scatter | solution.py:195
  9.6 12.4 %collective-permute-start.48 = (bf16[64,1000]{1,0:T(8,128)(2,1)}, bf16[64,1000]{1,0:T(8,128)(2,1)S(1)}, u32[]{:S(2)}, u32[]{:S(2)}) collective-permute-start(bf16[64,1000]{1,0:T(8,128)(2,1)} %dynamic-slice_bitcast_fusion.20), channel_id=1, source_target_pairs={{0,16},{16,0},{32,48},{48,32},{64,80},{80,64},{96,112},{112,96},{1... | collective-permute-start | bytes 384008 | tf_op jit(solution)/shard_map/ppermute | solution.py:48
  13.3 12.0 %collective-permute-start = (bf16[64,1000]{1,0:T(8,128)(2,1)}, bf16[64,1000]{1,0:T(8,128)(2,1)}, u32[]{:S(2)}, u32[]{:S(2)}) collective-permute-start(bf16[64,1000]{1,0:T(8,128)(2,1)} %get-tuple-element.48), channel_id=1, source_target_pairs={{0,1},{1,2},{2,3},{3,0},{4,5},{5,6},{6,7},{7,4},{8,9},{9,10},{10,1... | collective-permute-start | bytes 384008 | tf_op jit(solution)/shard_map/ppermute | solution.py:48
  14.6 11.4 %collective-permute-start.2 = (bf16[64,1000]{1,0:T(8,128)(2,1)}, bf16[64,1000]{1,0:T(8,128)(2,1)}, u32[]{:S(2)}, u32[]{:S(2)}) collective-permute-start(bf16[64,1000]{1,0:T(8,128)(2,1)} %get-tuple-element.49), channel_id=1, source_target_pairs={{0,3},{1,0},{2,1},{3,2},{4,7},{5,4},{6,5},{7,6},{8,11},{9,8},{10,9... | collective-permute-start | bytes 384008 | tf_op jit(solution)/shard_map/ppermute | solution.py:48
  16.0 10.0 %collective-permute-start.1 = (bf16[64,1000]{1,0:T(8,128)(2,1)}, bf16[64,1000]{1,0:T(8,128)(2,1)}, u32[]{:S(2)}, u32[]{:S(2)}) collective-permute-start(bf16[64,1000]{1,0:T(8,128)(2,1)} %get-tuple-element.50), channel_id=1, source_target_pairs={{0,2},{1,3},{2,0},{3,1},{4,6},{5,7},{6,4},{7,5},{8,10},{9,11},{10,... | collective-permute-start | bytes 384008 | tf_op jit(solution)/shard_map/ppermute | solution.py:48
  44.3 10.5 %collective-permute-start.53 = (bf16[64,1000]{1,0:T(8,128)(2,1)}, bf16[64,1000]{1,0:T(8,128)(2,1)S(1)}, u32[]{:S(2)}, u32[]{:S(2)}) collective-permute-start(bf16[64,1000]{1,0:T(8,128)(2,1)} %get-tuple-element.36), channel_id=1, source_target_pairs={{0,1},{1,2},{2,3},{3,0},{4,5},{5,6},{6,7},{7,4},{8,9},{9,10},{10,1... | collective-permute-start | bytes 384008 | tf_op jit(solution)/shard_map/ppermute | solution.py:48
  44.3 10.5 %collective-permute-start.55 = (bf16[64,1000]{1,0:T(8,128)(2,1)}, bf16[64,1000]{1,0:T(8,128)(2,1)S(1)}, u32[]{:S(2)}, u32[]{:S(2)}) collective-permute-start(bf16[64,1000]{1,0:T(8,128)(2,1)} %get-tuple-element.37), channel_id=1, source_target_pairs={{0,3},{1,0},{2,1},{3,2},{4,7},{5,4},{6,5},{7,6},{8,11},{9,8},{10,9... | collective-permute-start | bytes 384008 | tf_op jit(solution)/shard_map/ppermute | solution.py:48
  57.4 11.7 %collective-permute-start.12 = (bf16[64,1000]{1,0:T(8,128)(2,1)S(1)}, bf16[64,1000]{1,0:T(8,128)(2,1)S(1)}, u32[]{:S(2)}, u32[]{:S(2)}) collective-permute-start(bf16[64,1000]{1,0:T(8,128)(2,1)S(1)} %fusion.147), channel_id=1, source_target_pairs={{0,96},{16,112},{32,0},{48,16},{64,32},{80,48},{96,64},{112,80},{1... | collective-permute-start | bytes 384008 | tf_op jit(solution)/shard_map/ppermute | solution.py:37
  60.2 10.9 %collective-permute-start.11 = (bf16[64,1000]{1,0:T(8,128)(2,1)S(1)}, bf16[64,1000]{1,0:T(8,128)(2,1)S(1)}, u32[]{:S(2)}, u32[]{:S(2)}) collective-permute-start(bf16[64,1000]{1,0:T(8,128)(2,1)S(1)} %fusion.147), channel_id=1, source_target_pairs={{0,64},{16,80},{32,96},{48,112},{64,0},{80,16},{96,32},{112,48},{1... | collective-permute-start | bytes 384008 | tf_op jit(solution)/shard_map/ppermute | solution.py:37
  61.1 10.0 %collective-permute-start.10 = (bf16[64,1000]{1,0:T(8,128)(2,1)S(1)}, bf16[64,1000]{1,0:T(8,128)(2,1)S(1)}, u32[]{:S(2)}, u32[]{:S(2)}) collective-permute-start(bf16[64,1000]{1,0:T(8,128)(2,1)S(1)} %fusion.147), channel_id=1, source_target_pairs={{0,32},{16,48},{32,64},{48,80},{64,96},{80,112},{96,0},{112,16},{1... | collective-permute-start | bytes 384008 | tf_op jit(solution)/shard_map/ppermute | solution.py:37
  63.3 9.3 %collective-permute-start.61 = (bf16[64,1000]{1,0:T(8,128)(2,1)S(1)}, bf16[64,1000]{1,0:T(8,128)(2,1)S(1)}, u32[]{:S(2)}, u32[]{:S(2)}) collective-permute-start(bf16[64,1000]{1,0:T(8,128)(2,1)S(1)} %add_convert_fusion.5), channel_id=1, source_target_pairs={{0,1},{1,2},{2,3},{3,0},{4,5},{5,6},{6,7},{7,4},{8,9},{9,10},{10,1... | collective-permute-start | bytes 384008 | tf_op jit(solution)/shard_map/ppermute | solution.py:57
  65.5 9.4 %collective-permute-start.60 = (bf16[64,1000]{1,0:T(8,128)(2,1)S(1)}, bf16[64,1000]{1,0:T(8,128)(2,1)S(1)}, u32[]{:S(2)}, u32[]{:S(2)}) collective-permute-start(bf16[64,1000]{1,0:T(8,128)(2,1)S(1)} %add_convert_fusion.5), channel_id=1, source_target_pairs={{0,2},{1,3},{2,0},{3,1},{4,6},{5,7},{6,4},{7,5},{8,10},{9,11},{10,... | collective-permute-start | bytes 384008 | tf_op jit(solution)/shard_map/ppermute | solution.py:57
  115.4 16.3 %collective-permute-start.72 = (bf16[64,1000]{1,0:T(8,128)(2,1)S(1)}, bf16[64,1000]{1,0:T(8,128)(2,1)S(1)}, u32[]{:S(2)}, u32[]{:S(2)}) collective-permute-start(bf16[64,1000]{1,0:T(8,128)(2,1)S(1)} %fusion.130), channel_id=1, source_target_pairs={{0,12},{1,13},{2,14},{3,15},{4,0},{5,1},{6,2},{7,3},{8,4},{9,5},{1... | collective-permute-start | bytes 384008 | tf_op jit(solution)/shard_map/ppermute | solution.py:37
  135.2 13.0 %collective-permute-start.26 = (bf16[64,1000]{1,0:T(8,128)(2,1)S(1)}, bf16[64,1000]{1,0:T(8,128)(2,1)S(1)}, u32[]{:S(2)}, u32[]{:S(2)}) collective-permute-start(bf16[64,1000]{1,0:T(8,128)(2,1)S(1)} %fusion.143), channel_id=1, source_target_pairs={{0,96},{16,112},{32,0},{48,16},{64,32},{80,48},{96,64},{112,80},{1... | collective-permute-start | bytes 384008 | tf_op jit(solution)/shard_map/ppermute | solution.py:37
  137.9 10.4 %collective-permute-start.25 = (bf16[64,1000]{1,0:T(8,128)(2,1)S(1)}, bf16[64,1000]{1,0:T(8,128)(2,1)S(1)}, u32[]{:S(2)}, u32[]{:S(2)}) collective-permute-start(bf16[64,1000]{1,0:T(8,128)(2,1)S(1)} %fusion.143), channel_id=1, source_target_pairs={{0,64},{16,80},{32,96},{48,112},{64,0},{80,16},{96,32},{112,48},{1... | collective-permute-start | bytes 384008 | tf_op jit(solution)/shard_map/ppermute | solution.py:37
  138.6 9.7 %collective-permute-start.24 = (bf16[64,1000]{1,0:T(8,128)(2,1)S(1)}, bf16[64,1000]{1,0:T(8,128)(2,1)S(1)}, u32[]{:S(2)}, u32[]{:S(2)}) collective-permute-start(bf16[64,1000]{1,0:T(8,128)(2,1)S(1)} %fusion.143), channel_id=1, source_target_pairs={{0,32},{16,48},{32,64},{48,80},{64,96},{80,112},{96,0},{112,16},{1... | collective-permute-start | bytes 384008 | tf_op jit(solution)/shard_map/ppermute | solution.py:37
  142.1 9.3 %collective-permute-start.76 = (bf16[64,1000]{1,0:T(8,128)(2,1)S(1)}, bf16[64,1000]{1,0:T(8,128)(2,1)S(1)}, u32[]{:S(2)}, u32[]{:S(2)}) collective-permute-start(bf16[64,1000]{1,0:T(8,128)(2,1)S(1)} %dynamic-slice_bitcast_fusion.12), channel_id=1, source_target_pairs={{0,16},{16,0},{32,48},{48,32},{64,80},{80,64},{96,112},{112,96},{1... | collective-permute-start | bytes 384008 | tf_op jit(solution)/shard_map/ppermute | solution.py:48
  181.2 9.4 %collective-permute-start.84 = (bf16[64,1000]{1,0:T(8,128)(2,1)S(1)}, bf16[64,1000]{1,0:T(8,128)(2,1)S(1)}, u32[]{:S(2)}, u32[]{:S(2)}) collective-permute-start(bf16[64,1000]{1,0:T(8,128)(2,1)S(1)} %fusion.126), channel_id=1, source_target_pairs={{0,4},{1,5},{2,6},{3,7},{4,8},{5,9},{6,10},{7,11},{8,12},{9,13},{1... | collective-permute-start | bytes 384008 | tf_op jit(solution)/shard_map/ppermute | solution.py:37
  182.9 11.2 %collective-permute-start.36 = (bf16[64,1000]{1,0:T(8,128)(2,1)S(1)}, bf16[64,1000]{1,0:T(8,128)(2,1)S(1)}, u32[]{:S(2)}, u32[]{:S(2)}) collective-permute-start(bf16[64,1000]{1,0:T(8,128)(2,1)S(1)} %add_convert_fusion.9), channel_id=1, source_target_pairs={{0,1},{1,2},{2,3},{3,0},{4,5},{5,6},{6,7},{7,4},{8,9},{9,10},{10,1... | collective-permute-start | bytes 384008 | tf_op jit(solution)/shard_map/ppermute | solution.py:57
  241.5 9.8 %collective-permute-start.38 = (bf16[64,1000]{1,0:T(8,128)(2,1)S(1)}, bf16[64,1000]{1,0:T(8,128)(2,1)S(1)}, u32[]{:S(2)}, u32[]{:S(2)}) collective-permute-start(bf16[64,1000]{1,0:T(8,128)(2,1)S(1)} %fusion.139), channel_id=1, source_target_pairs={{0,32},{16,48},{32,64},{48,80},{64,96},{80,112},{96,0},{112,16},{1... | collective-permute-start | bytes 384008 | tf_op jit(solution)/shard_map/ppermute | solution.py:37
  254.5 9.3 %collective-permute-start.42 = (bf16[64,1000]{1,0:T(8,128)(2,1)S(1)}, bf16[64,1000]{1,0:T(8,128)(2,1)S(1)}, u32[]{:S(2)}, u32[]{:S(2)}) collective-permute-start(bf16[64,1000]{1,0:T(8,128)(2,1)S(1)} %get-tuple-element.39), channel_id=1, source_target_pairs={{0,1},{1,2},{2,3},{3,0},{4,5},{5,6},{6,7},{7,4},{8,9},{9,10},{10,1... | collective-permute-start | bytes 384008 | tf_op jit(solution)/shard_map/ppermute | solution.py:48
  257.2 12.9 %collective-permute-start.43 = (bf16[64,1000]{1,0:T(8,128)(2,1)S(1)}, bf16[64,1000]{1,0:T(8,128)(2,1)S(1)}, u32[]{:S(2)}, u32[]{:S(2)}) collective-permute-start(bf16[64,1000]{1,0:T(8,128)(2,1)S(1)} %get-tuple-element.41), channel_id=1, source_target_pairs={{0,2},{1,3},{2,0},{3,1},{4,6},{5,7},{6,4},{7,5},{8,10},{9,11},{10,... | collective-permute-start | bytes 384008 | tf_op jit(solution)/shard_map/ppermute | solution.py:48
  271.2 11.9 %collective-permute-start.45 = (bf16[64,1000]{1,0:T(8,128)(2,1)S(1)}, bf16[64,1000]{1,0:T(8,128)(2,1)S(1)}, u32[]{:S(2)}, u32[]{:S(2)}) collective-permute-start(bf16[64,1000]{1,0:T(8,128)(2,1)S(1)} %fusion.138), channel_id=1, source_target_pairs={{0,4},{1,5},{2,6},{3,7},{4,8},{5,9},{6,10},{7,11},{8,12},{9,13},{1... | collective-permute-start | bytes 384008 | tf_op jit(solution)/shard_map/ppermute | solution.py:37
  284.4 12.1 %collective-permute-start.96 = (bf16[64,1000]{1,0:T(8,128)(2,1)S(1)}, bf16[64,1000]{1,0:T(8,128)(2,1)S(1)}, u32[]{:S(2)}, u32[]{:S(2)}) collective-permute-start(bf16[64,1000]{1,0:T(8,128)(2,1)S(1)} %add_convert_fusion.7), channel_id=1, source_target_pairs={{0,2},{1,3},{2,0},{3,1},{4,6},{5,7},{6,4},{7,5},{8,10},{9,11},{10,... | collective-permute-start | bytes 384008 | tf_op jit(solution)/shard_map/ppermute | solution.py:57
  285.3 12.8 %collective-permute-start.95 = (bf16[64,1000]{1,0:T(8,128)(2,1)S(1)}, bf16[64,1000]{1,0:T(8,128)(2,1)S(1)}, u32[]{:S(2)}, u32[]{:S(2)}) collective-permute-start(bf16[64,1000]{1,0:T(8,128)(2,1)S(1)} %add_convert_fusion.7), channel_id=1, source_target_pairs={{0,3},{1,0},{2,1},{3,2},{4,7},{5,4},{6,5},{7,6},{8,11},{9,8},{10,9... | collective-permute-start | bytes 384008 | tf_op jit(solution)/shard_map/ppermute | solution.py:57
  310.7 15.4 %collective-permute-start.102 = (bf16[4,448,488]{2,1,0:T(8,128)(2,1)}, bf16[4,448,488]{2,1,0:T(8,128)(2,1)S(1)}, u32[]{:S(2)}, u32[]{:S(2)}) collective-permute-start(bf16[4,448,488]{2,1,0:T(8,128)(2,1)} %dynamic-slice_bitcast_fusion), channel_id=1, source_target_pairs={{0,16},{16,0},{32,48},{48,32},{64,80},{80,64},{96,112},{112,96},{1... | collective-permute-start | bytes 5246984 | tf_op jit(solution)/shard_map/ppermute | solution.py:72
  329.9 23.2 %collective-permute-start.103 = (bf16[448,488]{1,0:T(8,128)(2,1)S(1)}, bf16[448,488]{1,0:T(8,128)(2,1)S(1)}, u32[]{:S(2)}, u32[]{:S(2)}) collective-permute-start(bf16[448,488]{1,0:T(8,128)(2,1)S(1)} %get-tuple-element.24), channel_id=1, source_target_pairs={{0,32},{16,48},{32,64},{48,80},{64,96},{80,112},{96,0},{112,16},{1... | collective-permute-start | bytes 1311752 | tf_op jit(solution)/shard_map/ppermute | solution.py:81
  329.9 31.1 %collective-permute-start.105 = (bf16[448,488]{1,0:T(8,128)(2,1)}, bf16[448,488]{1,0:T(8,128)(2,1)}, u32[]{:S(2)}, u32[]{:S(2)}) collective-permute-start(bf16[448,488]{1,0:T(8,128)(2,1)} %get-tuple-element.25), channel_id=1, source_target_pairs={{0,96},{16,112},{32,0},{48,16},{64,32},{80,48},{96,64},{112,80},{1... | collective-permute-start | bytes 1311752 | tf_op jit(solution)/shard_map/ppermute | solution.py:81
  332.5 28.4 %collective-permute-start.104 = (bf16[448,488]{1,0:T(8,128)(2,1)}, bf16[448,488]{1,0:T(8,128)(2,1)}, u32[]{:S(2)}, u32[]{:S(2)}) collective-permute-start(bf16[448,488]{1,0:T(8,128)(2,1)} %get-tuple-element.26), channel_id=1, source_target_pairs={{0,64},{16,80},{32,96},{48,112},{64,0},{80,16},{96,32},{112,48},{1... | collective-permute-start | bytes 1311752 | tf_op jit(solution)/shard_map/ppermute | solution.py:81
  335.8 37.1 %collective-permute-start.99 = (bf16[448,512]{1,0:T(8,128)(2,1)}, bf16[448,512]{1,0:T(8,128)(2,1)}, u32[]{:S(2)}, u32[]{:S(2)}) collective-permute-start(bf16[448,512]{1,0:T(8,128)(2,1)} %get-tuple-element.21), channel_id=1, source_target_pairs={{0,32},{16,48},{32,64},{48,80},{64,96},{80,112},{96,0},{112,16},{1... | collective-permute-start | bytes 1376264 | tf_op jit(solution)/shard_map/ppermute | solution.py:81
  336.3 36.5 %collective-permute-start.101 = (bf16[448,512]{1,0:T(8,128)(2,1)}, bf16[448,512]{1,0:T(8,128)(2,1)}, u32[]{:S(2)}, u32[]{:S(2)}) collective-permute-start(bf16[448,512]{1,0:T(8,128)(2,1)} %get-tuple-element.22), channel_id=1, source_target_pairs={{0,96},{16,112},{32,0},{48,16},{64,32},{80,48},{96,64},{112,80},{1... | collective-permute-start | bytes 1376264 | tf_op jit(solution)/shard_map/ppermute | solution.py:81
  353.8 19.0 %collective-permute-start.100 = (bf16[448,512]{1,0:T(8,128)(2,1)}, bf16[448,512]{1,0:T(8,128)(2,1)}, u32[]{:S(2)}, u32[]{:S(2)}) collective-permute-start(bf16[448,512]{1,0:T(8,128)(2,1)} %get-tuple-element.23), channel_id=1, source_target_pairs={{0,64},{16,80},{32,96},{48,112},{64,0},{80,16},{96,32},{112,48},{1... | collective-permute-start | bytes 1376264 | tf_op jit(solution)/shard_map/ppermute | solution.py:81
  (96 other events, 784.1 us)
Sparse Core Ops, SparseCore 0:
  237.1 112.5 reduce-scatter.1
where the time goes:
time: 391 us; the launch traced here: 385 us
  starting transfers between devices  143 us (37%)
  waiting for transfers between devices  121 us (31%)
  matrix products  52.2 us (13%)
  other arithmetic  30.2 us (8%)
  local copies, waits for them, and re-layouts  24.4 us (6%)
  between operations  15.2 us (4%)
    ppermute x42, waiting for transfers between devices, ar_direct(): lax.ppermute(send, axis, shift_pairs(n, inner, sub, d)).astype(jnp.float32)  53.7 us
    ppermute x28, starting transfers between devices, rs_direct(): lax.ppermute(sel.astype(jnp.bfloat16), axis, shift_pairs(n, inner, sub, d))  47.9 us
    ppermute x42, starting transfers between devices, ar_direct(): lax.ppermute(send, axis, shift_pairs(n, inner, sub, d)).astype(jnp.float32)  45.7 us
    ppermute x28, starting transfers between devices, ag_direct(): lax.ppermute(p, axis, shift_pairs(n, inner, sub, -d))  39.9 us
    dot_general x14, matrix products, leading_dot(): lax.dot_general(left, right, (((0,), (0,)), ((), ())), preferred_element_...  28.4 us
    ppermute x6, waiting for transfers between devices, rs_hier(): lax.ppermute(sel, axis, shift_pairs(n, inner, 'outer', d))  24.8 us
    ppermute x28, waiting for transfers between devices, rs_direct(): lax.ppermute(sel.astype(jnp.bfloat16), axis, shift_pairs(n, inner, sub, d))  21.2 us
    ppermute x28, waiting for transfers between devices, ag_direct(): lax.ppermute(p, axis, shift_pairs(n, inner, sub, -d))  21 us
  transfers between devices with their start and end apart: 107, of which 44 were waited for; matrix products, arithmetic and copies ran while one was open for 20% of the time, Pallas kernels for 0%

commit v1 on v0

--- a/solution.py
+++ b/solution.py
@@ -125,6 +125,7 @@
         panel_index = panels - 1 - step
         if panel_index == panels - 1:
             shifted = backward_head[panel_index]
+            backward_lead = shifted
         else:
             summed = None
             for later_panel in range(panel_index + 1, panels):
@@ -133,6 +134,7 @@
                     block, upper_list[later_panel], preferred_element_type=jnp.float32
                 )
                 summed = product if summed is None else summed + product
+            backward_lead = summed
             pulled = reduce_col(summed).astype(jnp.float32)
             shifted = (backward_head[panel_index].astype(jnp.float32) - pulled).astype(jnp.bfloat16)
         upper_list[panel_index] = reduce_row(
@@ -155,7 +157,7 @@
             adjusted = (forward_head[panel_index].astype(jnp.float32) - coupling).astype(
                 jnp.bfloat16
             )
-        lead = shifted
+        lead = backward_lead
         if step == panels - 1:
             upper_head = jnp.stack(upper_list)
             panel_cols = upper_head.shape[1]

time: 391 us -> 398 us (1.018)
  waiting for transfers between devices: 121 us -> 133 us
  starting transfers between devices: 143 us -> 138 us
    ppermute x28, waiting for transfers between devices: 21.2 us -> 27.7 us  [rs_direct(): lax.ppermute(sel.astype(jnp.bfloat16), axis, shift_pairs(n, inner, sub, d))]
    ppermute x28, waiting for transfers between devices: 21 us -> 26.3 us  [ag_direct(): lax.ppermute(p, axis, shift_pairs(n, inner, sub, -d))]
    ppermute x28, starting transfers between devices: 39.9 us -> 34.9 us  [ag_direct(): lax.ppermute(p, axis, shift_pairs(n, inner, sub, -d))]
  transfers between devices with their start and end apart: 107 -> 107, of which waited for: 44 -> 53; matrix products, arithmetic and copies ran while one was open for 20% -> 20% of each run, Pallas kernels for 0% -> 0%
where the time goes in v1:
time: 398 us; the launch traced here: 392 us
  starting transfers between devices  138 us (35%)
  waiting for transfers between devices  133 us (33%)
  matrix products  52.3 us (13%)
  other arithmetic  29.2 us (7%)
  local copies, waits for them, and re-layouts  24.4 us (6%)
  between operations  15.2 us (4%)
    ppermute x42, waiting for transfers between devices, ar_direct(): lax.ppermute(send, axis, shift_pairs(n, inner, sub, d)).astype(jnp.float32)  54.4 us
    ppermute x42, starting transfers between devices, ar_direct(): lax.ppermute(send, axis, shift_pairs(n, inner, sub, d)).astype(jnp.float32)  47.3 us
    ppermute x28, starting transfers between devices, rs_direct(): lax.ppermute(sel.astype(jnp.bfloat16), axis, shift_pairs(n, inner, sub, d))  46.6 us
    ppermute x28, starting transfers between devices, ag_direct(): lax.ppermute(p, axis, shift_pairs(n, inner, sub, -d))  34.9 us
    dot_general x14, matrix products, leading_dot(): lax.dot_general(left, right, (((0,), (0,)), ((), ())), preferred_element_...  28.4 us
    ppermute x28, waiting for transfers between devices, rs_direct(): lax.ppermute(sel.astype(jnp.bfloat16), axis, shift_pairs(n, inner, sub, d))  27.7 us
    ppermute x28, waiting for transfers between devices, ag_direct(): lax.ppermute(p, axis, shift_pairs(n, inner, sub, -d))  26.3 us
    ppermute x6, waiting for transfers between devices, rs_hier(): lax.ppermute(sel, axis, shift_pairs(n, inner, 'outer', d))  24.8 us
  transfers between devices with their start and end apart: 107, of which 53 were waited for; matrix products, arithmetic and copies ran while one was open for 20% of the time, Pallas kernels for 0%

profile of v1, /device:TPU:1, one launch (start us, length us, event | category | flops | bytes accessed | tf_op | source)
XLA Modules:
  0.0 392.3 jit_solution(10376064873258707491)
XLA Ops:
  24.9 3.8 collective-permute-start.5
  29.5 2.8 collective-permute-start.17
  69.7 3.7 collective-permute-done.36
  100.6 3.6 collective-permute-done.43
  105.4 2.7 collective-permute-done.22
  119.5 2.7 collective-permute-done.62
  122.3 9.7 %collective-permute-start.66 = (bf16[64,1000]{1,0:T(8,128)(2,1)S(1)}, bf16[64,1000]{1,0:T(8,128)(2,1)S(1)}, u32[]{:S(2)}, u32[]{:S(2)}) collective-permute-start(bf16[64,1000]{1,0:T(8,128)(2,1)S(1)} %fusion.130), channel_id=1, source_target_pairs={{0,12},{1,13},{2,14},{3,15},{4,0},{5,1},{6,2},{7,3},{8,4},{9,5},{1... | collective-permute-start | bytes 384008 | tf_op jit(solution)/shard_map/ppermute | solution.py:37
  134.0 4.4 %collective-permute-start.28 = (bf16[64,1000]{1,0:T(8,128)(2,1)S(1)}, bf16[64,1000]{1,0:T(8,128)(2,1)S(1)}, u32[]{:S(2)}, u32[]{:S(2)}) collective-permute-start(bf16[64,1000]{1,0:T(8,128)(2,1)S(1)} %dynamic-slice_bitcast_fusion.27), channel_id=1, source_target_pairs={{0,16},{16,0},{32,48},{48,32},{64,80},{80,64},{96,112},{112,96},{1... | collective-permute-start | bytes 384008 | tf_op jit(solution)/shard_map/ppermute | solution.py:48
  148.0 6.8 %collective-permute-start.70 = (bf16[64,1000]{1,0:T(8,128)(2,1)S(1)}, bf16[64,1000]{1,0:T(8,128)(2,1)S(1)}, u32[]{:S(2)}, u32[]{:S(2)}) collective-permute-start(bf16[64,1000]{1,0:T(8,128)(2,1)S(1)} %dynamic-slice_bitcast_fusion.15), channel_id=1, source_target_pairs={{0,16},{16,0},{32,48},{48,32},{64,80},{80,64},{96,112},{112,96},{1... | collective-permute-start | bytes 384008 | tf_op jit(solution)/shard_map/ppermute | solution.py:48
  154.9 3.0 collective-permute-start.32
  165.4 3.4 collective-permute-done.71
  189.8 3.5 collective-permute-start.55
  201.3 2.8 collective-permute-done.89
  204.1 3.5 collective-permute-done.88
  211.5 3.6 collective-permute-start.90
  222.4 3.6 collective-permute-done.91
  229.7 14.1 %fusion = bf16[7168,1000]{1,0:T(8,128)(2,1)} fusion(bf16[4,128,1000]{1,2,0:T(8,128)(2,1)S(1)} %pad_maximum_fusion.2, bf16[7168,4,128]{2,1,0:T(4,128)(2,1)} %param.23), kind=kOutput, calls=%fused_computation.1 | convolution fusion | flops 7347200000 | bytes 22700032 | tf_op jit(solution)/shard_map/dot_general | solution.py:167
  254.2 3.8 collective-permute-done.57
  265.0 5.9 %collective-permute-done.75 = bf16[64,1000]{1,0:T(8,128)(2,1)S(1)} collective-permute-done((bf16[64,1000]{1,0:T(8,128)(2,1)S(1)}, bf16[64,1000]{1,0:T(8,128)(2,1)S(1)}, u32[]{:S(2)}, u32[]{:S(2)}) %collective-permute-start.75) | collective-permute-done | bytes 128032 | tf_op jit(solution)/shard_map/ppermute | solution.py:48
  270.9 6.1 %collective-permute-done.76 = bf16[64,1000]{1,0:T(8,128)(2,1)S(1)} collective-permute-done((bf16[64,1000]{1,0:T(8,128)(2,1)S(1)}, bf16[64,1000]{1,0:T(8,128)(2,1)S(1)}, u32[]{:S(2)}, u32[]{:S(2)}) %collective-permute-start.76) | collective-permute-done | bytes 128032 | tf_op jit(solution)/shard_map/ppermute | solution.py:48
  278.8 5.7 %collective-permute-done.80 = bf16[64,1000]{1,0:T(8,128)(2,1)S(1)} collective-permute-done((bf16[64,1000]{1,0:T(8,128)(2,1)S(1)}, bf16[64,1000]{1,0:T(8,128)(2,1)S(1)}, u32[]{:S(2)}, u32[]{:S(2)}) %collective-permute-start.80) | collective-permute-done | bytes 128032 | tf_op jit(solution)/shard_map/ppermute | solution.py:37
  286.0 3.9 %collective-permute-done.78 = bf16[64,1000]{1,0:T(8,128)(2,1)S(1)} collective-permute-done((bf16[64,1000]{1,0:T(8,128)(2,1)S(1)}, bf16[64,1000]{1,0:T(8,128)(2,1)S(1)}, u32[]{:S(2)}, u32[]{:S(2)}) %collective-permute-start.78) | collective-permute-done | bytes 128032 | tf_op jit(solution)/shard_map/ppermute | solution.py:37
  294.1 4.3 %collective-permute-done.97 = bf16[64,1000]{1,0:T(8,128)(2,1)S(1)} collective-permute-done((bf16[64,1000]{1,0:T(8,128)(2,1)S(1)}, bf16[64,1000]{1,0:T(8,128)(2,1)S(1)}, u32[]{:S(2)}, u32[]{:S(2)}) %collective-permute-start.97) | collective-permute-done | bytes 128032 | tf_op jit(solution)/shard_map/ppermute | solution.py:57
  298.5 4.9 %collective-permute-done.96 = bf16[64,1000]{1,0:T(8,128)(2,1)S(1)} collective-permute-done((bf16[64,1000]{1,0:T(8,128)(2,1)S(1)}, bf16[64,1000]{1,0:T(8,128)(2,1)S(1)}, u32[]{:S(2)}, u32[]{:S(2)}) %collective-permute-start.96) | collective-permute-done | bytes 128032 | tf_op jit(solution)/shard_map/ppermute | solution.py:57
  305.7 2.9 fusion.8
  308.6 7.5 %fusion.1 = bf16[3584,488]{1,0:T(8,128)(2,1)S(1)} fusion(f32[488,3584]{0,1:T(8,128)S(1)} %fusion.8, bf16[4,256,3584]{2,1,0:T(8,128)(2,1)} %param.18, bf16[3,256,1000]{2,1,0:T(8,128)(2,1)S(1)} %pad_maximum_fusion.1), kind=kOutput, calls=%fused_computation.3 | convolution fusion | flops 2689949696 | bytes 17129472 | tf_op jit(solution)/shard_map/dot_general | solution.py:103
  317.6 3.0 collective-permute-start.102
  320.6 2.7 fusion.10
  323.3 6.0 %fusion.2 = bf16[3584,512]{1,0:T(8,128)(2,1)S(1)} fusion(f32[512,3584]{0,1:T(8,128)S(1)} %fusion.10, bf16[4,256,3584]{2,1,0:T(8,128)(2,1)} %param.18, bf16[3,256,1000]{2,1,0:T(8,128)(2,1)S(1)} %pad_maximum_fusion.1), kind=kOutput, calls=%fused_computation.5 | convolution fusion | flops 2822242304 | bytes 19136512 | tf_op jit(solution)/shard_map/dot_general | solution.py:103
  333.1 2.7 fusion.5
  345.4 14.6 %collective-permute-done.103 = bf16[448,488]{1,0:T(8,128)(2,1)S(1)} collective-permute-done((bf16[448,488]{1,0:T(8,128)(2,1)S(1)}, bf16[448,488]{1,0:T(8,128)(2,1)S(1)}, u32[]{:S(2)}, u32[]{:S(2)}) %collective-permute-start.103) | collective-permute-done | bytes 437280 | tf_op jit(solution)/shard_map/ppermute | solution.py:81
  369.6 10.2 %collective-permute-done.99 = bf16[448,512]{1,0:T(8,128)(2,1)} collective-permute-done((bf16[448,512]{1,0:T(8,128)(2,1)}, bf16[448,512]{1,0:T(8,128)(2,1)}, u32[]{:S(2)}, u32[]{:S(2)}) %collective-permute-start.99) | collective-permute-done | bytes 458784 | tf_op jit(solution)/shard_map/ppermute | solution.py:81
  (347 shorter events, 215.0 us)
Async XLA Ops:
  7.2 375.7 %reduce-scatter.2.cloned.1.call-start = ((), (), s32[]{:S(2)}) async-start(), calls=%async_computation.1 | async-start | bytes 15597568 | tf_op jit(solution)/shard_map/reduce_scatter | solution.py:197
  9.6 19.9 %collective-permute-start.14 = (bf16[64,1000]{1,0:T(8,128)(2,1)}, bf16[64,1000]{1,0:T(8,128)(2,1)S(1)}, u32[]{:S(2)}, u32[]{:S(2)}) collective-permute-start(bf16[64,1000]{1,0:T(8,128)(2,1)} %dynamic-slice_bitcast_fusion.31), channel_id=1, source_target_pairs={{0,16},{16,0},{32,48},{48,32},{64,80},{80,64},{96,112},{112,96},{1... | collective-permute-start | bytes 384008 | tf_op jit(solution)/shard_map/ppermute | solution.py:48
  24.9 9.4 %collective-permute-start.5 = (bf16[64,1000]{1,0:T(8,128)(2,1)S(1)}, bf16[64,1000]{1,0:T(8,128)(2,1)S(1)}, u32[]{:S(2)}, u32[]{:S(2)}) collective-permute-start(bf16[64,1000]{1,0:T(8,128)(2,1)S(1)} %fusion.147), channel_id=1, source_target_pairs={{0,12},{1,13},{2,14},{3,15},{4,0},{5,1},{6,2},{7,3},{8,4},{9,5},{1... | collective-permute-start | bytes 384008 | tf_op jit(solution)/shard_map/ppermute | solution.py:37
  28.8 9.1 %collective-permute-start.3 = (bf16[64,1000]{1,0:T(8,128)(2,1)S(1)}, bf16[64,1000]{1,0:T(8,128)(2,1)S(1)}, u32[]{:S(2)}, u32[]{:S(2)}) collective-permute-start(bf16[64,1000]{1,0:T(8,128)(2,1)S(1)} %fusion.147), channel_id=1, source_target_pairs={{0,4},{1,5},{2,6},{3,7},{4,8},{5,9},{6,10},{7,11},{8,12},{9,13},{1... | collective-permute-start | bytes 384008 | tf_op jit(solution)/shard_map/ppermute | solution.py:37
  29.5 10.5 %collective-permute-start.17 = (bf16[64,1000]{1,0:T(8,128)(2,1)S(1)}, bf16[64,1000]{1,0:T(8,128)(2,1)S(1)}, u32[]{:S(2)}, u32[]{:S(2)}) collective-permute-start(bf16[64,1000]{1,0:T(8,128)(2,1)S(1)} %fusion.143), channel_id=1, source_target_pairs={{0,96},{16,112},{32,0},{48,16},{64,32},{80,48},{96,64},{112,80},{1... | collective-permute-start | bytes 384008 | tf_op jit(solution)/shard_map/ppermute | solution.py:37
  41.8 9.4 %collective-permute-start.18 = (bf16[64,1000]{1,0:T(8,128)(2,1)S(1)}, bf16[64,1000]{1,0:T(8,128)(2,1)S(1)}, u32[]{:S(2)}, u32[]{:S(2)}) collective-permute-start(bf16[64,1000]{1,0:T(8,128)(2,1)S(1)} %add_convert_fusion.11), channel_id=1, source_target_pairs={{0,16},{16,0},{32,48},{48,32},{64,80},{80,64},{96,112},{112,96},{1... | collective-permute-start | bytes 384008 | tf_op jit(solution)/shard_map/ppermute | solution.py:57
  49.4 15.6 %collective-permute-start.9 = (bf16[64,1000]{1,0:T(8,128)(2,1)}, bf16[64,1000]{1,0:T(8,128)(2,1)S(1)}, u32[]{:S(2)}, u32[]{:S(2)}) collective-permute-start(bf16[64,1000]{1,0:T(8,128)(2,1)} %dynamic-slice_bitcast_fusion.32), channel_id=1, source_target_pairs={{0,16},{16,0},{32,48},{48,32},{64,80},{80,64},{96,112},{112,96},{1... | collective-permute-start | bytes 384008 | tf_op jit(solution)/shard_map/ppermute | solution.py:48
  65.0 11.1 %collective-permute-start.12 = (bf16[64,1000]{1,0:T(8,128)(2,1)S(1)}, bf16[64,1000]{1,0:T(8,128)(2,1)S(1)}, u32[]{:S(2)}, u32[]{:S(2)}) collective-permute-start(bf16[64,1000]{1,0:T(8,128)(2,1)S(1)} %fusion.144), channel_id=1, source_target_pairs={{0,96},{16,112},{32,0},{48,16},{64,32},{80,48},{96,64},{112,80},{1... | collective-permute-start | bytes 384008 | tf_op jit(solution)/shard_map/ppermute | solution.py:37
  67.4 9.1 %collective-permute-start.11 = (bf16[64,1000]{1,0:T(8,128)(2,1)S(1)}, bf16[64,1000]{1,0:T(8,128)(2,1)S(1)}, u32[]{:S(2)}, u32[]{:S(2)}) collective-permute-start(bf16[64,1000]{1,0:T(8,128)(2,1)S(1)} %fusion.144), channel_id=1, source_target_pairs={{0,64},{16,80},{32,96},{48,112},{64,0},{80,16},{96,32},{112,48},{1... | collective-permute-start | bytes 384008 | tf_op jit(solution)/shard_map/ppermute | solution.py:37
  76.6 10.2 %collective-permute-start.13 = (bf16[64,1000]{1,0:T(8,128)(2,1)S(1)}, bf16[64,1000]{1,0:T(8,128)(2,1)S(1)}, u32[]{:S(2)}, u32[]{:S(2)}) collective-permute-start(bf16[64,1000]{1,0:T(8,128)(2,1)S(1)} %add_convert_fusion.12), channel_id=1, source_target_pairs={{0,16},{16,0},{32,48},{48,32},{64,80},{80,64},{96,112},{112,96},{1... | collective-permute-start | bytes 384008 | tf_op jit(solution)/shard_map/ppermute | solution.py:57
  98.8 9.3 %collective-permute-start.22 = (bf16[64,1000]{1,0:T(8,128)(2,1)S(1)}, bf16[64,1000]{1,0:T(8,128)(2,1)S(1)}, u32[]{:S(2)}, u32[]{:S(2)}) collective-permute-start(bf16[64,1000]{1,0:T(8,128)(2,1)S(1)} %fusion.142), channel_id=1, source_target_pairs={{0,4},{1,5},{2,6},{3,7},{4,8},{5,9},{6,10},{7,11},{8,12},{9,13},{1... | collective-permute-start | bytes 384008 | tf_op jit(solution)/shard_map/ppermute | solution.py:37
  108.5 9.2 %collective-permute-start.26 = (bf16[64,1000]{1,0:T(8,128)(2,1)S(1)}, bf16[64,1000]{1,0:T(8,128)(2,1)S(1)}, u32[]{:S(2)}, u32[]{:S(2)}) collective-permute-start(bf16[64,1000]{1,0:T(8,128)(2,1)S(1)} %add_convert_fusion.10), channel_id=1, source_target_pairs={{0,2},{1,3},{2,0},{3,1},{4,6},{5,7},{6,4},{7,5},{8,10},{9,11},{10,... | collective-permute-start | bytes 384008 | tf_op jit(solution)/shard_map/ppermute | solution.py:57
  122.3 16.2 %collective-permute-start.66 = (bf16[64,1000]{1,0:T(8,128)(2,1)S(1)}, bf16[64,1000]{1,0:T(8,128)(2,1)S(1)}, u32[]{:S(2)}, u32[]{:S(2)}) collective-permute-start(bf16[64,1000]{1,0:T(8,128)(2,1)S(1)} %fusion.130), channel_id=1, source_target_pairs={{0,12},{1,13},{2,14},{3,15},{4,0},{5,1},{6,2},{7,3},{8,4},{9,5},{1... | collective-permute-start | bytes 384008 | tf_op jit(solution)/shard_map/ppermute | solution.py:37
  142.2 12.5 %collective-permute-start.31 = (bf16[64,1000]{1,0:T(8,128)(2,1)S(1)}, bf16[64,1000]{1,0:T(8,128)(2,1)S(1)}, u32[]{:S(2)}, u32[]{:S(2)}) collective-permute-start(bf16[64,1000]{1,0:T(8,128)(2,1)S(1)} %fusion.139), channel_id=1, source_target_pairs={{0,96},{16,112},{32,0},{48,16},{64,32},{80,48},{96,64},{112,80},{1... | collective-permute-start | bytes 384008 | tf_op jit(solution)/shard_map/ppermute | solution.py:37
  144.6 10.2 %collective-permute-start.30 = (bf16[64,1000]{1,0:T(8,128)(2,1)S(1)}, bf16[64,1000]{1,0:T(8,128)(2,1)S(1)}, u32[]{:S(2)}, u32[]{:S(2)}) collective-permute-start(bf16[64,1000]{1,0:T(8,128)(2,1)S(1)} %fusion.139), channel_id=1, source_target_pairs={{0,64},{16,80},{32,96},{48,112},{64,0},{80,16},{96,32},{112,48},{1... | collective-permute-start | bytes 384008 | tf_op jit(solution)/shard_map/ppermute | solution.py:37
  145.5 9.3 %collective-permute-start.29 = (bf16[64,1000]{1,0:T(8,128)(2,1)S(1)}, bf16[64,1000]{1,0:T(8,128)(2,1)S(1)}, u32[]{:S(2)}, u32[]{:S(2)}) collective-permute-start(bf16[64,1000]{1,0:T(8,128)(2,1)S(1)} %fusion.139), channel_id=1, source_target_pairs={{0,32},{16,48},{32,64},{48,80},{64,96},{80,112},{96,0},{112,16},{1... | collective-permute-start | bytes 384008 | tf_op jit(solution)/shard_map/ppermute | solution.py:37
  148.0 9.9 %collective-permute-start.70 = (bf16[64,1000]{1,0:T(8,128)(2,1)S(1)}, bf16[64,1000]{1,0:T(8,128)(2,1)S(1)}, u32[]{:S(2)}, u32[]{:S(2)}) collective-permute-start(bf16[64,1000]{1,0:T(8,128)(2,1)S(1)} %dynamic-slice_bitcast_fusion.15), channel_id=1, source_target_pairs={{0,16},{16,0},{32,48},{48,32},{64,80},{80,64},{96,112},{112,96},{1... | collective-permute-start | bytes 384008 | tf_op jit(solution)/shard_map/ppermute | solution.py:48
  159.3 9.4 %collective-permute-start.71 = (bf16[64,1000]{1,0:T(8,128)(2,1)S(1)}, bf16[64,1000]{1,0:T(8,128)(2,1)S(1)}, u32[]{:S(2)}, u32[]{:S(2)}) collective-permute-start(bf16[64,1000]{1,0:T(8,128)(2,1)S(1)} %fusion.127), channel_id=1, source_target_pairs={{0,32},{16,48},{32,64},{48,80},{64,96},{80,112},{96,0},{112,16},{1... | collective-permute-start | bytes 384008 | tf_op jit(solution)/shard_map/ppermute | solution.py:37
  188.0 9.5 %collective-permute-start.84 = (bf16[64,1000]{1,0:T(8,128)(2,1)S(1)}, bf16[64,1000]{1,0:T(8,128)(2,1)S(1)}, u32[]{:S(2)}, u32[]{:S(2)}) collective-permute-start(bf16[64,1000]{1,0:T(8,128)(2,1)S(1)} %fusion.123), channel_id=1, source_target_pairs={{0,4},{1,5},{2,6},{3,7},{4,8},{5,9},{6,10},{7,11},{8,12},{9,13},{1... | collective-permute-start | bytes 384008 | tf_op jit(solution)/shard_map/ppermute | solution.py:37
  189.8 11.2 %collective-permute-start.55 = (bf16[64,1000]{1,0:T(8,128)(2,1)S(1)}, bf16[64,1000]{1,0:T(8,128)(2,1)S(1)}, u32[]{:S(2)}, u32[]{:S(2)}) collective-permute-start(bf16[64,1000]{1,0:T(8,128)(2,1)S(1)} %add_convert_fusion.6), channel_id=1, source_target_pairs={{0,1},{1,2},{2,3},{3,0},{4,5},{5,6},{6,7},{7,4},{8,9},{9,10},{10,1... | collective-permute-start | bytes 384008 | tf_op jit(solution)/shard_map/ppermute | solution.py:57
  261.3 9.5 %collective-permute-start.75 = (bf16[64,1000]{1,0:T(8,128)(2,1)S(1)}, bf16[64,1000]{1,0:T(8,128)(2,1)S(1)}, u32[]{:S(2)}, u32[]{:S(2)}) collective-permute-start(bf16[64,1000]{1,0:T(8,128)(2,1)S(1)} %get-tuple-element.39), channel_id=1, source_target_pairs={{0,1},{1,2},{2,3},{3,0},{4,5},{5,6},{6,7},{7,4},{8,9},{9,10},{10,1... | collective-permute-start | bytes 384008 | tf_op jit(solution)/shard_map/ppermute | solution.py:48
  264.0 12.9 %collective-permute-start.76 = (bf16[64,1000]{1,0:T(8,128)(2,1)S(1)}, bf16[64,1000]{1,0:T(8,128)(2,1)S(1)}, u32[]{:S(2)}, u32[]{:S(2)}) collective-permute-start(bf16[64,1000]{1,0:T(8,128)(2,1)S(1)} %get-tuple-element.41), channel_id=1, source_target_pairs={{0,2},{1,3},{2,0},{3,1},{4,6},{5,7},{6,4},{7,5},{8,10},{9,11},{10,... | collective-permute-start | bytes 384008 | tf_op jit(solution)/shard_map/ppermute | solution.py:48
  278.0 11.9 %collective-permute-start.78 = (bf16[64,1000]{1,0:T(8,128)(2,1)S(1)}, bf16[64,1000]{1,0:T(8,128)(2,1)S(1)}, u32[]{:S(2)}, u32[]{:S(2)}) collective-permute-start(bf16[64,1000]{1,0:T(8,128)(2,1)S(1)} %fusion.126), channel_id=1, source_target_pairs={{0,4},{1,5},{2,6},{3,7},{4,8},{5,9},{6,10},{7,11},{8,12},{9,13},{1... | collective-permute-start | bytes 384008 | tf_op jit(solution)/shard_map/ppermute | solution.py:37
  291.3 12.1 %collective-permute-start.96 = (bf16[64,1000]{1,0:T(8,128)(2,1)S(1)}, bf16[64,1000]{1,0:T(8,128)(2,1)S(1)}, u32[]{:S(2)}, u32[]{:S(2)}) collective-permute-start(bf16[64,1000]{1,0:T(8,128)(2,1)S(1)} %add_convert_fusion.2), channel_id=1, source_target_pairs={{0,2},{1,3},{2,0},{3,1},{4,6},{5,7},{6,4},{7,5},{8,10},{9,11},{10,... | collective-permute-start | bytes 384008 | tf_op jit(solution)/shard_map/ppermute | solution.py:57
  292.2 12.8 %collective-permute-start.95 = (bf16[64,1000]{1,0:T(8,128)(2,1)S(1)}, bf16[64,1000]{1,0:T(8,128)(2,1)S(1)}, u32[]{:S(2)}, u32[]{:S(2)}) collective-permute-start(bf16[64,1000]{1,0:T(8,128)(2,1)S(1)} %add_convert_fusion.2), channel_id=1, source_target_pairs={{0,3},{1,0},{2,1},{3,2},{4,7},{5,4},{6,5},{7,6},{8,11},{9,8},{10,9... | collective-permute-start | bytes 384008 | tf_op jit(solution)/shard_map/ppermute | solution.py:57
  317.6 15.5 %collective-permute-start.102 = (bf16[4,448,488]{2,1,0:T(8,128)(2,1)}, bf16[4,448,488]{2,1,0:T(8,128)(2,1)S(1)}, u32[]{:S(2)}, u32[]{:S(2)}) collective-permute-start(bf16[4,448,488]{2,1,0:T(8,128)(2,1)} %dynamic-slice_bitcast_fusion), channel_id=1, source_target_pairs={{0,16},{16,0},{32,48},{48,32},{64,80},{80,64},{96,112},{112,96},{1... | collective-permute-start | bytes 5246984 | tf_op jit(solution)/shard_map/ppermute | solution.py:72
  336.9 23.2 %collective-permute-start.103 = (bf16[448,488]{1,0:T(8,128)(2,1)S(1)}, bf16[448,488]{1,0:T(8,128)(2,1)S(1)}, u32[]{:S(2)}, u32[]{:S(2)}) collective-permute-start(bf16[448,488]{1,0:T(8,128)(2,1)S(1)} %get-tuple-element.30), channel_id=1, source_target_pairs={{0,32},{16,48},{32,64},{48,80},{64,96},{80,112},{96,0},{112,16},{1... | collective-permute-start | bytes 1311752 | tf_op jit(solution)/shard_map/ppermute | solution.py:81
  336.9 31.1 %collective-permute-start.105 = (bf16[448,488]{1,0:T(8,128)(2,1)}, bf16[448,488]{1,0:T(8,128)(2,1)}, u32[]{:S(2)}, u32[]{:S(2)}) collective-permute-start(bf16[448,488]{1,0:T(8,128)(2,1)} %get-tuple-element.31), channel_id=1, source_target_pairs={{0,96},{16,112},{32,0},{48,16},{64,32},{80,48},{96,64},{112,80},{1... | collective-permute-start | bytes 1311752 | tf_op jit(solution)/shard_map/ppermute | solution.py:81
  339.5 28.4 %collective-permute-start.104 = (bf16[448,488]{1,0:T(8,128)(2,1)}, bf16[448,488]{1,0:T(8,128)(2,1)}, u32[]{:S(2)}, u32[]{:S(2)}) collective-permute-start(bf16[448,488]{1,0:T(8,128)(2,1)} %get-tuple-element.32), channel_id=1, source_target_pairs={{0,64},{16,80},{32,96},{48,112},{64,0},{80,16},{96,32},{112,48},{1... | collective-permute-start | bytes 1311752 | tf_op jit(solution)/shard_map/ppermute | solution.py:81
  342.7 37.1 %collective-permute-start.99 = (bf16[448,512]{1,0:T(8,128)(2,1)}, bf16[448,512]{1,0:T(8,128)(2,1)}, u32[]{:S(2)}, u32[]{:S(2)}) collective-permute-start(bf16[448,512]{1,0:T(8,128)(2,1)} %get-tuple-element.27), channel_id=1, source_target_pairs={{0,32},{16,48},{32,64},{48,80},{64,96},{80,112},{96,0},{112,16},{1... | collective-permute-start | bytes 1376264 | tf_op jit(solution)/shard_map/ppermute | solution.py:81
  343.3 36.5 %collective-permute-start.101 = (bf16[448,512]{1,0:T(8,128)(2,1)}, bf16[448,512]{1,0:T(8,128)(2,1)}, u32[]{:S(2)}, u32[]{:S(2)}) collective-permute-start(bf16[448,512]{1,0:T(8,128)(2,1)} %get-tuple-element.28), channel_id=1, source_target_pairs={{0,96},{16,112},{32,0},{48,16},{64,32},{80,48},{96,64},{112,80},{1... | collective-permute-start | bytes 1376264 | tf_op jit(solution)/shard_map/ppermute | solution.py:81
  360.8 19.0 %collective-permute-start.100 = (bf16[448,512]{1,0:T(8,128)(2,1)}, bf16[448,512]{1,0:T(8,128)(2,1)}, u32[]{:S(2)}, u32[]{:S(2)}) collective-permute-start(bf16[448,512]{1,0:T(8,128)(2,1)} %get-tuple-element.29), channel_id=1, source_target_pairs={{0,64},{16,80},{32,96},{48,112},{64,0},{80,16},{96,32},{112,48},{1... | collective-permute-start | bytes 1376264 | tf_op jit(solution)/shard_map/ppermute | solution.py:81
  (96 other events, 771.2 us)
Sparse Core Ops, SparseCore 0:
  244.0 112.4 reduce-scatter.1

commit v2 on v0

--- a/solution.py
+++ b/solution.py
@@ -182,9 +182,11 @@
             continue
         part = lower_head[:, :, lo:hi]
         early_partial = with_layout_constraint(
-            leading_dot(early_slab, part[:early].reshape(early * panel_rows, hi - lo)),
+            leading_dot(early_slab, part[:early].reshape(early * panel_rows, hi - lo)).astype(
+                jnp.bfloat16
+            ),
             Layout(major_to_minor=(0, 1)),
-        )
+        ).astype(jnp.float32)
         lower_partial = with_layout_constraint(
             (early_partial + leading_dot(forward_slab[early], part[early])).astype(jnp.bfloat16),
             Layout(major_to_minor=(0, 1)),

time: 391 us -> 379 us (0.969)
  waiting for transfers between devices: 121 us -> 109 us
    ppermute x42, waiting for transfers between devices: 53.7 us -> 47.6 us  [ar_direct(): lax.ppermute(send, axis, shift_pairs(n, inner, sub, d)).astype(jnp.float32)]
    dot_general x14, matrix products: 28.4 us -> 22.8 us  [leading_dot(): lax.dot_general(left, right, (((0,), (0,)), ((), ())), preferred_element_...]
    unnamed x49 -> x57, local copies, waits for them, and re-layouts: 8.99 us -> 11 us
  transfers between devices with their start and end apart: 107 -> 107, of which waited for: 44 -> 40; matrix products, arithmetic and copies ran while one was open for 20% -> 21% of each run, Pallas kernels for 0% -> 0%
where the time goes in v2:
time: 379 us; the launch traced here: 373 us
  starting transfers between devices  141 us (37%)
  waiting for transfers between devices  109 us (29%)
  matrix products  49.1 us (13%)
  other arithmetic  31.8 us (8%)
  local copies, waits for them, and re-layouts  26.6 us (7%)
  between operations  15.2 us (4%)
    ppermute x28, starting transfers between devices, rs_direct(): lax.ppermute(sel.astype(jnp.bfloat16), axis, shift_pairs(n, inner, sub, d))  49 us
    ppermute x42, waiting for transfers between devices, ar_direct(): lax.ppermute(send, axis, shift_pairs(n, inner, sub, d)).astype(jnp.float32)  47.6 us
    ppermute x42, starting transfers between devices, ar_direct(): lax.ppermute(send, axis, shift_pairs(n, inner, sub, d)).astype(jnp.float32)  46.7 us
    ppermute x28, starting transfers between devices, ag_direct(): lax.ppermute(p, axis, shift_pairs(n, inner, sub, -d))  38 us
    ppermute x6, waiting for transfers between devices, rs_hier(): lax.ppermute(sel, axis, shift_pairs(n, inner, 'outer', d))  24 us
    dot_general x14, matrix products, leading_dot(): lax.dot_general(left, right, (((0,), (0,)), ((), ())), preferred_element_...  22.8 us
    ppermute x28, waiting for transfers between devices, rs_direct(): lax.ppermute(sel.astype(jnp.bfloat16), axis, shift_pairs(n, inner, sub, d))  19.9 us
    ppermute x28, waiting for transfers between devices, ag_direct(): lax.ppermute(p, axis, shift_pairs(n, inner, sub, -d))  17.5 us
  transfers between devices with their start and end apart: 107, of which 40 were waited for; matrix products, arithmetic and copies ran while one was open for 21% of the time, Pallas kernels for 0%

profile of v2, /device:TPU:1, one launch (start us, length us, event | category | flops | bytes accessed | tf_op | source)
XLA Modules:
  0.0 373.0 jit_solution(1254951077790958256)
XLA Ops:
  23.1 2.8 collective-permute-start.51
  28.1 3.8 %collective-permute-start.5 = (bf16[64,1000]{1,0:T(8,128)(2,1)S(1)}, bf16[64,1000]{1,0:T(8,128)(2,1)S(1)}, u32[]{:S(2)}, u32[]{:S(2)}) collective-permute-start(bf16[64,1000]{1,0:T(8,128)(2,1)S(1)} %fusion.152), channel_id=1, source_target_pairs={{0,12},{1,13},{2,14},{3,15},{4,0},{5,1},{6,2},{7,3},{8,4},{9,5},{1... | collective-permute-start | bytes 384008 | tf_op jit(solution)/shard_map/ppermute | solution.py:37
  50.4 4.3 %collective-permute-start.9 = (bf16[64,1000]{1,0:T(8,128)(2,1)S(1)}, bf16[64,1000]{1,0:T(8,128)(2,1)S(1)}, u32[]{:S(2)}, u32[]{:S(2)}) collective-permute-start(bf16[64,1000]{1,0:T(8,128)(2,1)S(1)} %dynamic-slice_bitcast_fusion.32), channel_id=1, source_target_pairs={{0,16},{16,0},{32,48},{48,32},{64,80},{80,64},{96,112},{112,96},{1... | collective-permute-start | bytes 384008 | tf_op jit(solution)/shard_map/ppermute | solution.py:48
  58.5 2.8 collective-permute-start.12
  66.4 3.8 %collective-permute-start.60 = (bf16[64,1000]{1,0:T(8,128)(2,1)S(1)}, bf16[64,1000]{1,0:T(8,128)(2,1)S(1)}, u32[]{:S(2)}, u32[]{:S(2)}) collective-permute-start(bf16[64,1000]{1,0:T(8,128)(2,1)S(1)} %add_convert_fusion.5), channel_id=1, source_target_pairs={{0,2},{1,3},{2,0},{3,1},{4,6},{5,7},{6,4},{7,5},{8,10},{9,11},{10,... | collective-permute-start | bytes 384008 | tf_op jit(solution)/shard_map/ppermute | solution.py:57
  95.3 3.6 collective-permute-done.63
  102.5 2.9 collective-permute-start.21
  113.7 2.8 collective-permute-done.68
  116.6 9.6 %collective-permute-start.72 = (bf16[64,1000]{1,0:T(8,128)(2,1)S(1)}, bf16[64,1000]{1,0:T(8,128)(2,1)}, u32[]{:S(2)}, u32[]{:S(2)}) collective-permute-start(bf16[64,1000]{1,0:T(8,128)(2,1)S(1)} %fusion.132), channel_id=1, source_target_pairs={{0,12},{1,13},{2,14},{3,15},{4,0},{5,1},{6,2},{7,3},{8,4},{9,5},{1... | collective-permute-start | bytes 384008 | tf_op jit(solution)/shard_map/ppermute | solution.py:37
  128.5 4.6 %collective-permute-start.23 = (bf16[64,1000]{1,0:T(8,128)(2,1)S(1)}, bf16[64,1000]{1,0:T(8,128)(2,1)S(1)}, u32[]{:S(2)}, u32[]{:S(2)}) collective-permute-start(bf16[64,1000]{1,0:T(8,128)(2,1)S(1)} %dynamic-slice_bitcast_fusion.28), channel_id=1, source_target_pairs={{0,16},{16,0},{32,48},{48,32},{64,80},{80,64},{96,112},{112,96},{1... | collective-permute-start | bytes 384008 | tf_op jit(solution)/shard_map/ppermute | solution.py:48
  137.4 2.9 collective-permute-start.26
  144.3 6.2 %collective-permute-start.76 = (bf16[64,1000]{1,0:T(8,128)(2,1)S(1)}, bf16[64,1000]{1,0:T(8,128)(2,1)S(1)}, u32[]{:S(2)}, u32[]{:S(2)}) collective-permute-start(bf16[64,1000]{1,0:T(8,128)(2,1)S(1)} %dynamic-slice_bitcast_fusion.12), channel_id=1, source_target_pairs={{0,16},{16,0},{32,48},{48,32},{64,80},{80,64},{96,112},{112,96},{1... | collective-permute-start | bytes 384008 | tf_op jit(solution)/shard_map/ppermute | solution.py:48
  150.6 3.0 collective-permute-start.27
  156.0 2.8 collective-permute-done.79
  160.7 3.4 collective-permute-done.77
  200.3 3.5 collective-permute-done.88
  203.8 2.7 fusion.56
  208.0 5.3 %collective-permute-start.90 = (bf16[64,1000]{1,0:T(8,128)(2,1)S(1)}, bf16[64,1000]{1,0:T(8,128)(2,1)S(1)}, u32[]{:S(2)}, u32[]{:S(2)}) collective-permute-start(bf16[64,1000]{1,0:T(8,128)(2,1)S(1)} %dynamic-slice_bitcast_fusion.8), channel_id=1, source_target_pairs={{0,16},{16,0},{32,48},{48,32},{64,80},{80,64},{96,112},{112,96},{1... | collective-permute-start | bytes 384008 | tf_op jit(solution)/shard_map/ppermute | solution.py:48
  215.9 3.3 collective-permute-done.93
  221.0 3.8 %collective-permute-done.91 = bf16[64,1000]{1,0:T(8,128)(2,1)S(1)} collective-permute-done((bf16[64,1000]{1,0:T(8,128)(2,1)S(1)}, bf16[64,1000]{1,0:T(8,128)(2,1)S(1)}, u32[]{:S(2)}, u32[]{:S(2)}) %collective-permute-start.91) | collective-permute-done | bytes 128032 | tf_op jit(solution)/shard_map/ppermute | solution.py:37
  228.4 14.1 %fusion = bf16[7168,1000]{1,0:T(8,128)(2,1)} fusion(bf16[4,128,1000]{1,2,0:T(8,128)(2,1)S(1)} %pad_maximum_fusion.2, bf16[7168,4,128]{2,1,0:T(4,128)(2,1)} %param.23), kind=kOutput, calls=%fused_computation.1 | convolution fusion | flops 7347200000 | bytes 22700032 | tf_op jit(solution)/shard_map/dot_general | solution.py:165
  247.8 3.4 collective-permute-done.40
  252.5 3.8 %collective-permute-done.38 = bf16[64,1000]{1,0:T(8,128)(2,1)S(1)} collective-permute-done((bf16[64,1000]{1,0:T(8,128)(2,1)S(1)}, bf16[64,1000]{1,0:T(8,128)(2,1)S(1)}, u32[]{:S(2)}, u32[]{:S(2)}) %collective-permute-start.38) | collective-permute-done | bytes 128032 | tf_op jit(solution)/shard_map/ppermute | solution.py:37
  262.5 6.3 %collective-permute-done.42 = bf16[64,1000]{1,0:T(8,128)(2,1)S(1)} collective-permute-done((bf16[64,1000]{1,0:T(8,128)(2,1)S(1)}, bf16[64,1000]{1,0:T(8,128)(2,1)S(1)}, u32[]{:S(2)}, u32[]{:S(2)}) %collective-permute-start.42) | collective-permute-done | bytes 128032 | tf_op jit(solution)/shard_map/ppermute | solution.py:48
  268.8 5.8 %collective-permute-done.43 = bf16[64,1000]{1,0:T(8,128)(2,1)S(1)} collective-permute-done((bf16[64,1000]{1,0:T(8,128)(2,1)S(1)}, bf16[64,1000]{1,0:T(8,128)(2,1)S(1)}, u32[]{:S(2)}, u32[]{:S(2)}) %collective-permute-start.43) | collective-permute-done | bytes 128032 | tf_op jit(solution)/shard_map/ppermute | solution.py:48
  276.6 7.5 %fusion.5 = bf16[3584,488]{1,0:T(8,128)(2,1)S(1)} fusion(bf16[4,256,3584]{2,1,0:T(8,128)(2,1)} %param.18, bf16[3,256,1000]{2,1,0:T(8,128)(2,1)S(1)} %pad_maximum_fusion.1), kind=kOutput, calls=%fused_computation.10 | convolution fusion | flops 2688200704 | bytes 9789440 | tf_op jit(solution)/shard_map/dot_general | solution.py:103
  284.1 3.8 %collective-permute-done.45 = bf16[64,1000]{1,0:T(8,128)(2,1)S(1)} collective-permute-done((bf16[64,1000]{1,0:T(8,128)(2,1)S(1)}, bf16[64,1000]{1,0:T(8,128)(2,1)S(1)}, u32[]{:S(2)}, u32[]{:S(2)}) %collective-permute-start.45) | collective-permute-done | bytes 128032 | tf_op jit(solution)/shard_map/ppermute | solution.py:37
  291.1 3.3 fusion.8
  296.5 5.0 %collective-permute-done.96 = bf16[64,1000]{1,0:T(8,128)(2,1)S(1)} collective-permute-done((bf16[64,1000]{1,0:T(8,128)(2,1)S(1)}, bf16[64,1000]{1,0:T(8,128)(2,1)S(1)}, u32[]{:S(2)}, u32[]{:S(2)}) %collective-permute-start.96) | collective-permute-done | bytes 128032 | tf_op jit(solution)/shard_map/ppermute | solution.py:57
  314.3 2.8 fusion.9
  327.0 13.0 %collective-permute-done.103 = bf16[448,488]{1,0:T(8,128)(2,1)S(1)} collective-permute-done((bf16[448,488]{1,0:T(8,128)(2,1)S(1)}, bf16[448,488]{1,0:T(8,128)(2,1)S(1)}, u32[]{:S(2)}, u32[]{:S(2)}) %collective-permute-start.103) | collective-permute-done | bytes 437280 | tf_op jit(solution)/shard_map/ppermute | solution.py:81
  349.5 11.0 %collective-permute-done.99 = bf16[448,512]{1,0:T(8,128)(2,1)} collective-permute-done((bf16[448,512]{1,0:T(8,128)(2,1)}, bf16[448,512]{1,0:T(8,128)(2,1)}, u32[]{:S(2)}, u32[]{:S(2)}) %collective-permute-start.99) | collective-permute-done | bytes 458784 | tf_op jit(solution)/shard_map/ppermute | solution.py:81
  (356 shorter events, 200.1 us)
Async XLA Ops:
  7.2 356.3 %reduce-scatter.2.cloned.1.call-start = ((), (), s32[]{:S(2)}) async-start(), calls=%async_computation.1 | async-start | bytes 15597568 | tf_op jit(solution)/shard_map/reduce_scatter | solution.py:197
  9.6 13.4 %collective-permute-start.48 = (bf16[64,1000]{1,0:T(8,128)(2,1)}, bf16[64,1000]{1,0:T(8,128)(2,1)S(1)}, u32[]{:S(2)}, u32[]{:S(2)}) collective-permute-start(bf16[64,1000]{1,0:T(8,128)(2,1)} %dynamic-slice_bitcast_fusion.20), channel_id=1, source_target_pairs={{0,16},{16,0},{32,48},{48,32},{64,80},{80,64},{96,112},{112,96},{1... | collective-permute-start | bytes 384008 | tf_op jit(solution)/shard_map/ppermute | solution.py:48
  13.3 12.9 %collective-permute-start = (bf16[64,1000]{1,0:T(8,128)(2,1)}, bf16[64,1000]{1,0:T(8,128)(2,1)}, u32[]{:S(2)}, u32[]{:S(2)}) collective-permute-start(bf16[64,1000]{1,0:T(8,128)(2,1)} %get-tuple-element.48), channel_id=1, source_target_pairs={{0,1},{1,2},{2,3},{3,0},{4,5},{5,6},{6,7},{7,4},{8,9},{9,10},{10,1... | collective-permute-start | bytes 384008 | tf_op jit(solution)/shard_map/ppermute | solution.py:48
  14.6 12.4 %collective-permute-start.2 = (bf16[64,1000]{1,0:T(8,128)(2,1)}, bf16[64,1000]{1,0:T(8,128)(2,1)}, u32[]{:S(2)}, u32[]{:S(2)}) collective-permute-start(bf16[64,1000]{1,0:T(8,128)(2,1)} %get-tuple-element.49), channel_id=1, source_target_pairs={{0,3},{1,0},{2,1},{3,2},{4,7},{5,4},{6,5},{7,6},{8,11},{9,8},{10,9... | collective-permute-start | bytes 384008 | tf_op jit(solution)/shard_map/ppermute | solution.py:48
  16.0 11.0 %collective-permute-start.1 = (bf16[64,1000]{1,0:T(8,128)(2,1)}, bf16[64,1000]{1,0:T(8,128)(2,1)}, u32[]{:S(2)}, u32[]{:S(2)}) collective-permute-start(bf16[64,1000]{1,0:T(8,128)(2,1)} %get-tuple-element.50), channel_id=1, source_target_pairs={{0,2},{1,3},{2,0},{3,1},{4,6},{5,7},{6,4},{7,5},{8,10},{9,11},{10,... | collective-permute-start | bytes 384008 | tf_op jit(solution)/shard_map/ppermute | solution.py:48
  45.3 10.5 %collective-permute-start.53 = (bf16[64,1000]{1,0:T(8,128)(2,1)}, bf16[64,1000]{1,0:T(8,128)(2,1)S(1)}, u32[]{:S(2)}, u32[]{:S(2)}) collective-permute-start(bf16[64,1000]{1,0:T(8,128)(2,1)} %get-tuple-element.36), channel_id=1, source_target_pairs={{0,1},{1,2},{2,3},{3,0},{4,5},{5,6},{6,7},{7,4},{8,9},{9,10},{10,1... | collective-permute-start | bytes 384008 | tf_op jit(solution)/shard_map/ppermute | solution.py:48
  45.3 10.5 %collective-permute-start.55 = (bf16[64,1000]{1,0:T(8,128)(2,1)}, bf16[64,1000]{1,0:T(8,128)(2,1)}, u32[]{:S(2)}, u32[]{:S(2)}) collective-permute-start(bf16[64,1000]{1,0:T(8,128)(2,1)} %get-tuple-element.37), channel_id=1, source_target_pairs={{0,3},{1,0},{2,1},{3,2},{4,7},{5,4},{6,5},{7,6},{8,11},{9,8},{10,9... | collective-permute-start | bytes 384008 | tf_op jit(solution)/shard_map/ppermute | solution.py:48
  58.5 11.7 %collective-permute-start.12 = (bf16[64,1000]{1,0:T(8,128)(2,1)S(1)}, bf16[64,1000]{1,0:T(8,128)(2,1)S(1)}, u32[]{:S(2)}, u32[]{:S(2)}) collective-permute-start(bf16[64,1000]{1,0:T(8,128)(2,1)S(1)} %fusion.149), channel_id=1, source_target_pairs={{0,96},{16,112},{32,0},{48,16},{64,32},{80,48},{96,64},{112,80},{1... | collective-permute-start | bytes 384008 | tf_op jit(solution)/shard_map/ppermute | solution.py:37
  61.4 10.9 %collective-permute-start.11 = (bf16[64,1000]{1,0:T(8,128)(2,1)S(1)}, bf16[64,1000]{1,0:T(8,128)(2,1)S(1)}, u32[]{:S(2)}, u32[]{:S(2)}) collective-permute-start(bf16[64,1000]{1,0:T(8,128)(2,1)S(1)} %fusion.149), channel_id=1, source_target_pairs={{0,64},{16,80},{32,96},{48,112},{64,0},{80,16},{96,32},{112,48},{1... | collective-permute-start | bytes 384008 | tf_op jit(solution)/shard_map/ppermute | solution.py:37
  62.2 10.0 %collective-permute-start.10 = (bf16[64,1000]{1,0:T(8,128)(2,1)S(1)}, bf16[64,1000]{1,0:T(8,128)(2,1)S(1)}, u32[]{:S(2)}, u32[]{:S(2)}) collective-permute-start(bf16[64,1000]{1,0:T(8,128)(2,1)S(1)} %fusion.149), channel_id=1, source_target_pairs={{0,32},{16,48},{32,64},{48,80},{64,96},{80,112},{96,0},{112,16},{1... | collective-permute-start | bytes 384008 | tf_op jit(solution)/shard_map/ppermute | solution.py:37
  66.4 9.5 %collective-permute-start.60 = (bf16[64,1000]{1,0:T(8,128)(2,1)S(1)}, bf16[64,1000]{1,0:T(8,128)(2,1)S(1)}, u32[]{:S(2)}, u32[]{:S(2)}) collective-permute-start(bf16[64,1000]{1,0:T(8,128)(2,1)S(1)} %add_convert_fusion.5), channel_id=1, source_target_pairs={{0,2},{1,3},{2,0},{3,1},{4,6},{5,7},{6,4},{7,5},{8,10},{9,11},{10,... | collective-permute-start | bytes 384008 | tf_op jit(solution)/shard_map/ppermute | solution.py:57
  116.6 16.5 %collective-permute-start.72 = (bf16[64,1000]{1,0:T(8,128)(2,1)S(1)}, bf16[64,1000]{1,0:T(8,128)(2,1)}, u32[]{:S(2)}, u32[]{:S(2)}) collective-permute-start(bf16[64,1000]{1,0:T(8,128)(2,1)S(1)} %fusion.132), channel_id=1, source_target_pairs={{0,12},{1,13},{2,14},{3,15},{4,0},{5,1},{6,2},{7,3},{8,4},{9,5},{1... | collective-permute-start | bytes 384008 | tf_op jit(solution)/shard_map/ppermute | solution.py:37
  137.4 13.0 %collective-permute-start.26 = (bf16[64,1000]{1,0:T(8,128)(2,1)S(1)}, bf16[64,1000]{1,0:T(8,128)(2,1)S(1)}, u32[]{:S(2)}, u32[]{:S(2)}) collective-permute-start(bf16[64,1000]{1,0:T(8,128)(2,1)S(1)} %fusion.145), channel_id=1, source_target_pairs={{0,96},{16,112},{32,0},{48,16},{64,32},{80,48},{96,64},{112,80},{1... | collective-permute-start | bytes 384008 | tf_op jit(solution)/shard_map/ppermute | solution.py:37
  140.3 10.2 %collective-permute-start.25 = (bf16[64,1000]{1,0:T(8,128)(2,1)S(1)}, bf16[64,1000]{1,0:T(8,128)(2,1)S(1)}, u32[]{:S(2)}, u32[]{:S(2)}) collective-permute-start(bf16[64,1000]{1,0:T(8,128)(2,1)S(1)} %fusion.145), channel_id=1, source_target_pairs={{0,64},{16,80},{32,96},{48,112},{64,0},{80,16},{96,32},{112,48},{1... | collective-permute-start | bytes 384008 | tf_op jit(solution)/shard_map/ppermute | solution.py:37
  140.8 9.6 %collective-permute-start.24 = (bf16[64,1000]{1,0:T(8,128)(2,1)S(1)}, bf16[64,1000]{1,0:T(8,128)(2,1)S(1)}, u32[]{:S(2)}, u32[]{:S(2)}) collective-permute-start(bf16[64,1000]{1,0:T(8,128)(2,1)S(1)} %fusion.145), channel_id=1, source_target_pairs={{0,32},{16,48},{32,64},{48,80},{64,96},{80,112},{96,0},{112,16},{1... | collective-permute-start | bytes 384008 | tf_op jit(solution)/shard_map/ppermute | solution.py:37
  166.9 10.1 %collective-permute-start.28 = (bf16[64,1000]{1,0:T(8,128)(2,1)}, bf16[64,1000]{1,0:T(8,128)(2,1)S(1)}, u32[]{:S(2)}, u32[]{:S(2)}) collective-permute-start(bf16[64,1000]{1,0:T(8,128)(2,1)} %get-tuple-element.42), channel_id=1, source_target_pairs={{0,1},{1,2},{2,3},{3,0},{4,5},{5,6},{6,7},{7,4},{8,9},{9,10},{10,1... | collective-permute-start | bytes 384008 | tf_op jit(solution)/shard_map/ppermute | solution.py:48
  167.2 10.9 %collective-permute-start.30 = (bf16[64,1000]{1,0:T(8,128)(2,1)}, bf16[64,1000]{1,0:T(8,128)(2,1)}, u32[]{:S(2)}, u32[]{:S(2)}) collective-permute-start(bf16[64,1000]{1,0:T(8,128)(2,1)} %get-tuple-element.43), channel_id=1, source_target_pairs={{0,3},{1,0},{2,1},{3,2},{4,7},{5,4},{6,5},{7,6},{8,11},{9,8},{10,9... | collective-permute-start | bytes 384008 | tf_op jit(solution)/shard_map/ppermute | solution.py:48
  188.9 9.7 %collective-permute-start.35 = (bf16[64,1000]{1,0:T(8,128)(2,1)S(1)}, bf16[64,1000]{1,0:T(8,128)(2,1)S(1)}, u32[]{:S(2)}, u32[]{:S(2)}) collective-permute-start(bf16[64,1000]{1,0:T(8,128)(2,1)S(1)} %add_convert_fusion.9), channel_id=1, source_target_pairs={{0,2},{1,3},{2,0},{3,1},{4,6},{5,7},{6,4},{7,5},{8,10},{9,11},{10,... | collective-permute-start | bytes 384008 | tf_op jit(solution)/shard_map/ppermute | solution.py:57
  215.1 9.7 %collective-permute-start.91 = (bf16[64,1000]{1,0:T(8,128)(2,1)S(1)}, bf16[64,1000]{1,0:T(8,128)(2,1)S(1)}, u32[]{:S(2)}, u32[]{:S(2)}) collective-permute-start(bf16[64,1000]{1,0:T(8,128)(2,1)S(1)} %fusion.125), channel_id=1, source_target_pairs={{0,32},{16,48},{32,64},{48,80},{64,96},{80,112},{96,0},{112,16},{1... | collective-permute-start | bytes 384008 | tf_op jit(solution)/shard_map/ppermute | solution.py:37
  246.6 9.7 %collective-permute-start.38 = (bf16[64,1000]{1,0:T(8,128)(2,1)S(1)}, bf16[64,1000]{1,0:T(8,128)(2,1)S(1)}, u32[]{:S(2)}, u32[]{:S(2)}) collective-permute-start(bf16[64,1000]{1,0:T(8,128)(2,1)S(1)} %fusion.141), channel_id=1, source_target_pairs={{0,32},{16,48},{32,64},{48,80},{64,96},{80,112},{96,0},{112,16},{1... | collective-permute-start | bytes 384008 | tf_op jit(solution)/shard_map/ppermute | solution.py:37
  262.3 12.3 %collective-permute-start.43 = (bf16[64,1000]{1,0:T(8,128)(2,1)S(1)}, bf16[64,1000]{1,0:T(8,128)(2,1)S(1)}, u32[]{:S(2)}, u32[]{:S(2)}) collective-permute-start(bf16[64,1000]{1,0:T(8,128)(2,1)S(1)} %get-tuple-element.41), channel_id=1, source_target_pairs={{0,2},{1,3},{2,0},{3,1},{4,6},{5,7},{6,4},{7,5},{8,10},{9,11},{10,... | collective-permute-start | bytes 384008 | tf_op jit(solution)/shard_map/ppermute | solution.py:48
  274.7 9.4 %collective-permute-start.47 = (bf16[64,1000]{1,0:T(8,128)(2,1)S(1)}, bf16[64,1000]{1,0:T(8,128)(2,1)S(1)}, u32[]{:S(2)}, u32[]{:S(2)}) collective-permute-start(bf16[64,1000]{1,0:T(8,128)(2,1)S(1)} %fusion.140), channel_id=1, source_target_pairs={{0,12},{1,13},{2,14},{3,15},{4,0},{5,1},{6,2},{7,3},{8,4},{9,5},{1... | collective-permute-start | bytes 384008 | tf_op jit(solution)/shard_map/ppermute | solution.py:37
  274.8 9.4 %collective-permute-start.46 = (bf16[64,1000]{1,0:T(8,128)(2,1)S(1)}, bf16[64,1000]{1,0:T(8,128)(2,1)S(1)}, u32[]{:S(2)}, u32[]{:S(2)}) collective-permute-start(bf16[64,1000]{1,0:T(8,128)(2,1)S(1)} %fusion.140), channel_id=1, source_target_pairs={{0,8},{1,9},{2,10},{3,11},{4,12},{5,13},{6,14},{7,15},{8,0},{9,1},... | collective-permute-start | bytes 384008 | tf_op jit(solution)/shard_map/ppermute | solution.py:37
  275.7 12.2 %collective-permute-start.45 = (bf16[64,1000]{1,0:T(8,128)(2,1)S(1)}, bf16[64,1000]{1,0:T(8,128)(2,1)S(1)}, u32[]{:S(2)}, u32[]{:S(2)}) collective-permute-start(bf16[64,1000]{1,0:T(8,128)(2,1)S(1)} %fusion.140), channel_id=1, source_target_pairs={{0,4},{1,5},{2,6},{3,7},{4,8},{5,9},{6,10},{7,11},{8,12},{9,13},{1... | collective-permute-start | bytes 384008 | tf_op jit(solution)/shard_map/ppermute | solution.py:37
  288.6 13.0 %collective-permute-start.96 = (bf16[64,1000]{1,0:T(8,128)(2,1)S(1)}, bf16[64,1000]{1,0:T(8,128)(2,1)S(1)}, u32[]{:S(2)}, u32[]{:S(2)}) collective-permute-start(bf16[64,1000]{1,0:T(8,128)(2,1)S(1)} %add_convert_fusion.7), channel_id=1, source_target_pairs={{0,2},{1,3},{2,0},{3,1},{4,6},{5,7},{6,4},{7,5},{8,10},{9,11},{10,... | collective-permute-start | bytes 384008 | tf_op jit(solution)/shard_map/ppermute | solution.py:57
  290.2 13.0 %collective-permute-start.95 = (bf16[64,1000]{1,0:T(8,128)(2,1)S(1)}, bf16[64,1000]{1,0:T(8,128)(2,1)S(1)}, u32[]{:S(2)}, u32[]{:S(2)}) collective-permute-start(bf16[64,1000]{1,0:T(8,128)(2,1)S(1)} %add_convert_fusion.7), channel_id=1, source_target_pairs={{0,3},{1,0},{2,1},{3,2},{4,7},{5,4},{6,5},{7,6},{8,11},{9,8},{10,9... | collective-permute-start | bytes 384008 | tf_op jit(solution)/shard_map/ppermute | solution.py:57
  318.1 21.8 %collective-permute-start.103 = (bf16[448,488]{1,0:T(8,128)(2,1)S(1)}, bf16[448,488]{1,0:T(8,128)(2,1)S(1)}, u32[]{:S(2)}, u32[]{:S(2)}) collective-permute-start(bf16[448,488]{1,0:T(8,128)(2,1)S(1)} %get-tuple-element.24), channel_id=1, source_target_pairs={{0,32},{16,48},{32,64},{48,80},{64,96},{80,112},{96,0},{112,16},{1... | collective-permute-start | bytes 1311752 | tf_op jit(solution)/shard_map/ppermute | solution.py:81
  318.1 29.6 %collective-permute-start.105 = (bf16[448,488]{1,0:T(8,128)(2,1)}, bf16[448,488]{1,0:T(8,128)(2,1)}, u32[]{:S(2)}, u32[]{:S(2)}) collective-permute-start(bf16[448,488]{1,0:T(8,128)(2,1)} %get-tuple-element.25), channel_id=1, source_target_pairs={{0,96},{16,112},{32,0},{48,16},{64,32},{80,48},{96,64},{112,80},{1... | collective-permute-start | bytes 1311752 | tf_op jit(solution)/shard_map/ppermute | solution.py:81
  320.8 27.0 %collective-permute-start.104 = (bf16[448,488]{1,0:T(8,128)(2,1)}, bf16[448,488]{1,0:T(8,128)(2,1)}, u32[]{:S(2)}, u32[]{:S(2)}) collective-permute-start(bf16[448,488]{1,0:T(8,128)(2,1)} %get-tuple-element.26), channel_id=1, source_target_pairs={{0,64},{16,80},{32,96},{48,112},{64,0},{80,16},{96,32},{112,48},{1... | collective-permute-start | bytes 1311752 | tf_op jit(solution)/shard_map/ppermute | solution.py:81
  324.1 36.4 %collective-permute-start.99 = (bf16[448,512]{1,0:T(8,128)(2,1)}, bf16[448,512]{1,0:T(8,128)(2,1)}, u32[]{:S(2)}, u32[]{:S(2)}) collective-permute-start(bf16[448,512]{1,0:T(8,128)(2,1)} %get-tuple-element.21), channel_id=1, source_target_pairs={{0,32},{16,48},{32,64},{48,80},{64,96},{80,112},{96,0},{112,16},{1... | collective-permute-start | bytes 1376264 | tf_op jit(solution)/shard_map/ppermute | solution.py:81
  324.6 35.9 %collective-permute-start.101 = (bf16[448,512]{1,0:T(8,128)(2,1)}, bf16[448,512]{1,0:T(8,128)(2,1)}, u32[]{:S(2)}, u32[]{:S(2)}) collective-permute-start(bf16[448,512]{1,0:T(8,128)(2,1)} %get-tuple-element.22), channel_id=1, source_target_pairs={{0,96},{16,112},{32,0},{48,16},{64,32},{80,48},{96,64},{112,80},{1... | collective-permute-start | bytes 1376264 | tf_op jit(solution)/shard_map/ppermute | solution.py:81
  340.7 19.8 %collective-permute-start.100 = (bf16[448,512]{1,0:T(8,128)(2,1)}, bf16[448,512]{1,0:T(8,128)(2,1)}, u32[]{:S(2)}, u32[]{:S(2)}) collective-permute-start(bf16[448,512]{1,0:T(8,128)(2,1)} %get-tuple-element.23), channel_id=1, source_target_pairs={{0,64},{16,80},{32,96},{48,112},{64,0},{80,16},{96,32},{112,48},{1... | collective-permute-start | bytes 1376264 | tf_op jit(solution)/shard_map/ppermute | solution.py:81
  (100 other events, 834.8 us)
Sparse Core Ops, SparseCore 0:
  242.7 111.6 reduce-scatter.1

commit v3 on v2

--- a/solution.py
+++ b/solution.py
@@ -175,7 +175,7 @@
     panel_rows = lower_head.shape[1]
     early = panels - 1
     early_slab = forward_slab[:early].reshape(early * panel_rows, forward_slab.shape[2])
-    split = 512 if classes > 512 else classes
+    split = classes
     updates = []
     for lo, hi in ((0, split), (split, classes)):
         if hi <= lo:

time: 379 us -> 388 us (1.024)
  waiting for transfers between devices: 109 us -> 127 us
  starting transfers between devices: 141 us -> 137 us
    ppermute x6 -> x3, waiting for transfers between devices: 24 us -> 32.9 us  [rs_hier(): lax.ppermute(sel, axis, shift_pairs(n, inner, 'outer', d))]
    ppermute x42, waiting for transfers between devices: 47.6 us -> 54.5 us  [ar_direct(): lax.ppermute(send, axis, shift_pairs(n, inner, sub, d)).astype(jnp.float32)]
    ppermute x2 -> x1, waiting for transfers between devices: 0.01 us -> 6.38 us  [rs_hier(): lax.ppermute(sel, axis, shift_pairs(n, inner, 'inner', d))]
    ppermute x28, waiting for transfers between devices: 17.5 us -> 11.6 us  [ag_direct(): lax.ppermute(p, axis, shift_pairs(n, inner, sub, -d))]
    unnamed x57 -> x35, local copies, waits for them, and re-layouts: 11 us -> 9.73 us
    dot_general x14 -> x12, matrix products: 22.8 us -> 22.2 us  [leading_dot(): lax.dot_general(left, right, (((0,), (0,)), ((), ())), preferred_element_...]
  transfers between devices with their start and end apart: 107 -> 103, of which waited for: 40 -> 43; matrix products, arithmetic and copies ran while one was open for 21% -> 20% of each run, Pallas kernels for 0% -> 0%
where the time goes in v3:
time: 388 us; the launch traced here: 383 us
  starting transfers between devices  137 us (35%)
  waiting for transfers between devices  127 us (33%)
  matrix products  46.1 us (12%)
  other arithmetic  32 us (8%)
  local copies, waits for them, and re-layouts  25 us (6%)
  between operations  15.2 us (4%)
    ppermute x42, waiting for transfers between devices, ar_direct(): lax.ppermute(send, axis, shift_pairs(n, inner, sub, d)).astype(jnp.float32)  54.5 us
    ppermute x28, starting transfers between devices, rs_direct(): lax.ppermute(sel.astype(jnp.bfloat16), axis, shift_pairs(n, inner, sub, d))  48.6 us
    ppermute x42, starting transfers between devices, ar_direct(): lax.ppermute(send, axis, shift_pairs(n, inner, sub, d)).astype(jnp.float32)  43.7 us
    ppermute x28, starting transfers between devices, ag_direct(): lax.ppermute(p, axis, shift_pairs(n, inner, sub, -d))  39.2 us
    ppermute x3, waiting for transfers between devices, rs_hier(): lax.ppermute(sel, axis, shift_pairs(n, inner, 'outer', d))  32.9 us
    dot_general x12, matrix products, leading_dot(): lax.dot_general(left, right, (((0,), (0,)), ((), ())), preferred_element_...  22.2 us
    ppermute x28, waiting for transfers between devices, rs_direct(): lax.ppermute(sel.astype(jnp.bfloat16), axis, shift_pairs(n, inner, sub, d))  22.1 us
    dot_general x1, matrix products, local(): jnp.dot(flat_back, flat_upper, preferred_element_type=jnp.float32)  14.2 us
  transfers between devices with their start and end apart: 103, of which 43 were waited for; matrix products, arithmetic and copies ran while one was open for 20% of the time, Pallas kernels for 0%

profile of v3, /device:TPU:1, one launch (start us, length us, event | category | flops | bytes accessed | tf_op | source)
XLA Modules:
  0.0 383.0 jit_solution(13535815988837217389)
XLA Ops:
  23.1 2.8 collective-permute-start.51
  28.0 3.8 collective-permute-start.5
  50.3 4.3 %collective-permute-start.9 = (bf16[64,1000]{1,0:T(8,128)(2,1)S(1)}, bf16[64,1000]{1,0:T(8,128)(2,1)S(1)}, u32[]{:S(2)}, u32[]{:S(2)}) collective-permute-start(bf16[64,1000]{1,0:T(8,128)(2,1)S(1)} %dynamic-slice_bitcast_fusion.28), channel_id=1, source_target_pairs={{0,16},{16,0},{32,48},{48,32},{64,80},{80,64},{96,112},{112,96},{1... | collective-permute-start | bytes 384008 | tf_op jit(solution)/shard_map/ppermute | solution.py:48
  58.5 2.8 collective-permute-start.12
  66.4 3.8 collective-permute-start.60
  94.4 3.6 collective-permute-done.63
  99.4 3.2 collective-permute-done.17
  116.7 9.5 %collective-permute-start.72 = (bf16[64,1000]{1,0:T(8,128)(2,1)S(1)}, bf16[64,1000]{1,0:T(8,128)(2,1)S(1)}, u32[]{:S(2)}, u32[]{:S(2)}) collective-permute-start(bf16[64,1000]{1,0:T(8,128)(2,1)S(1)} %fusion.125), channel_id=1, source_target_pairs={{0,12},{1,13},{2,14},{3,15},{4,0},{5,1},{6,2},{7,3},{8,4},{9,5},{1... | collective-permute-start | bytes 384008 | tf_op jit(solution)/shard_map/ppermute | solution.py:37
  128.5 3.7 collective-permute-start.23
  143.3 7.1 %collective-permute-start.76 = (bf16[64,1000]{1,0:T(8,128)(2,1)S(1)}, bf16[64,1000]{1,0:T(8,128)(2,1)S(1)}, u32[]{:S(2)}, u32[]{:S(2)}) collective-permute-start(bf16[64,1000]{1,0:T(8,128)(2,1)S(1)} %dynamic-slice_bitcast_fusion.8), channel_id=1, source_target_pairs={{0,16},{16,0},{32,48},{48,32},{64,80},{80,64},{96,112},{112,96},{1... | collective-permute-start | bytes 384008 | tf_op jit(solution)/shard_map/ppermute | solution.py:48
  157.0 2.8 collective-permute-done.79
  161.2 3.5 collective-permute-done.77
  185.3 2.9 collective-permute-start.36
  197.1 4.4 %collective-permute-done.89 = bf16[64,1000]{1,0:T(8,128)(2,1)} collective-permute-done((bf16[64,1000]{1,0:T(8,128)(2,1)S(1)}, bf16[64,1000]{1,0:T(8,128)(2,1)}, u32[]{:S(2)}, u32[]{:S(2)}) %collective-permute-start.89) | collective-permute-done | bytes 128032 | tf_op jit(solution)/shard_map/ppermute | solution.py:57
  207.1 4.6 %collective-permute-start.90 = (bf16[64,1000]{1,0:T(8,128)(2,1)S(1)}, bf16[64,1000]{1,0:T(8,128)(2,1)S(1)}, u32[]{:S(2)}, u32[]{:S(2)}) collective-permute-start(bf16[64,1000]{1,0:T(8,128)(2,1)S(1)} %dynamic-slice_bitcast_fusion.4), channel_id=1, source_target_pairs={{0,16},{16,0},{32,48},{48,32},{64,80},{80,64},{96,112},{112,96},{1... | collective-permute-start | bytes 384008 | tf_op jit(solution)/shard_map/ppermute | solution.py:48
  214.2 3.3 collective-permute-done.93
  219.0 3.5 collective-permute-done.91
  226.1 14.2 %fusion.1 = bf16[7168,1000]{1,0:T(8,128)(2,1)} fusion(bf16[4,128,1000]{1,2,0:T(8,128)(2,1)S(1)} %pad_maximum_fusion.1, bf16[7168,4,128]{2,1,0:T(4,128)(2,1)} %param.23), kind=kOutput, calls=%fused_computation.4 | convolution fusion | flops 7347200000 | bytes 22700032 | tf_op jit(solution)/shard_map/dot_general | solution.py:165
  245.5 3.4 collective-permute-done.40
  250.7 3.8 collective-permute-done.38
  260.6 7.0 %collective-permute-done.42 = bf16[64,1000]{1,0:T(8,128)(2,1)S(1)} collective-permute-done((bf16[64,1000]{1,0:T(8,128)(2,1)S(1)}, bf16[64,1000]{1,0:T(8,128)(2,1)S(1)}, u32[]{:S(2)}, u32[]{:S(2)}) %collective-permute-start.42) | collective-permute-done | bytes 128032 | tf_op jit(solution)/shard_map/ppermute | solution.py:48
  267.6 4.9 %collective-permute-done.43 = bf16[64,1000]{1,0:T(8,128)(2,1)S(1)} collective-permute-done((bf16[64,1000]{1,0:T(8,128)(2,1)S(1)}, bf16[64,1000]{1,0:T(8,128)(2,1)S(1)}, u32[]{:S(2)}, u32[]{:S(2)}) %collective-permute-start.43) | collective-permute-done | bytes 128032 | tf_op jit(solution)/shard_map/ppermute | solution.py:48
  274.8 5.4 %collective-permute-done.47 = bf16[64,1000]{1,0:T(8,128)(2,1)S(1)} collective-permute-done((bf16[64,1000]{1,0:T(8,128)(2,1)S(1)}, bf16[64,1000]{1,0:T(8,128)(2,1)S(1)}, u32[]{:S(2)}, u32[]{:S(2)}) %collective-permute-start.47) | collective-permute-done | bytes 128032 | tf_op jit(solution)/shard_map/ppermute | solution.py:37
  281.7 3.9 %collective-permute-done.45 = bf16[64,1000]{1,0:T(8,128)(2,1)} collective-permute-done((bf16[64,1000]{1,0:T(8,128)(2,1)S(1)}, bf16[64,1000]{1,0:T(8,128)(2,1)}, u32[]{:S(2)}, u32[]{:S(2)}) %collective-permute-start.45) | collective-permute-done | bytes 128032 | tf_op jit(solution)/shard_map/ppermute | solution.py:37
  290.6 8.9 %bitcast_convert_fusion.1 = bf16[1000,3584]{0,1:T(8,128)(2,1)S(1)} fusion(bf16[4,256,3584]{2,1,0:T(8,128)(2,1)} %param.18, bf16[1,256,1000]{1,2,0:T(8,128)(2,1)S(1)} %copy.57, bf16[1,256,1000]{1,2,0:T(8,128)(2,1)S(1)} %copy.56, bf16[1,256,1000]{1,2,0:T(8,128)(2,1)S(1)} %copy.55), kind=kOutput, calls=%fused_computation.3 | convolution fusion | flops 5510144000 | bytes 14209024 | tf_op jit(solution)/shard_map/dot_general | solution.py:103
  302.1 4.0 %fusion = bf16[3584,1000]{1,0:T(8,128)(2,1)S(1)} fusion(bf16[256,1000]{1,0:T(8,128)(2,1)S(1)} %bitcast.356, bf16[1000,3584]{0,1:T(8,128)(2,1)S(1)} %bitcast_convert_fusion.1, bf16[4,256,3584]{2,1,0:T(8,128)(2,1)} %param.18), kind=kOutput, calls=%fused_computation.2 | convolution fusion | flops 1845760000 | bytes 16683008 | tf_op jit(solution)/shard_map/dot_general | solution.py:103
  310.4 3.0 collective-permute-start.98
  313.4 6.4 %collective-permute-done.98 = bf16[4,448,1000]{2,1,0:T(8,128)(2,1)} collective-permute-done((bf16[4,448,1000]{2,1,0:T(8,128)(2,1)}, bf16[4,448,1000]{2,1,0:T(8,128)(2,1)}, u32[]{:S(2)}, u32[]{:S(2)}) %collective-permute-start.98) | collective-permute-done | bytes 3584032 | tf_op jit(solution)/shard_map/ppermute | solution.py:72
  319.8 5.2 %fusion.2 = bf16[4,448,1000]{2,1,0:T(8,128)(2,1)S(1)} fusion(bf16[4,2,448,1000]{3,2,1,0:T(8,128)(2,1)} %bitcast.338, s32[]{:T(128)S(6)} %select_n.251, bf16[4,448,1000]{2,1,0:T(8,128)(2,1)} %collective-permute-done.98), kind=kLoop, calls=%fused_computation.6 | loop fusion | flops 7168000 | bytes 10752004 | tf_op jit(solution)/shard_map/convert_element_type | solution.py:75
  333.5 3.0 convert_element_type.889
  336.5 32.9 %collective-permute-done.99 = bf16[448,1000]{1,0:T(8,128)(2,1)} collective-permute-done((bf16[448,1000]{1,0:T(8,128)(2,1)}, bf16[448,1000]{1,0:T(8,128)(2,1)}, u32[]{:S(2)}, u32[]{:S(2)}) %collective-permute-start.99) | collective-permute-done | bytes 896032 | tf_op jit(solution)/shard_map/ppermute | solution.py:81
  369.4 4.1 %fusion.9 = bf16[448,1000]{1,0:T(8,128)(2,1)} fusion(bf16[448,1000]{1,0:T(8,128)(2,1)} %collective-permute-done.101, bf16[448,1000]{1,0:T(8,128)(2,1)} %collective-permute-done.100, bf16[448,1000]{1,0:T(8,128)(2,1)} %collective-permute-done.99, f32[4,448,1000]{2,1,0:T(8,128)S(1)} %convert_element_type.889, s32[]{:T(128)S(6)} %select_n.255, ...), kind=kLoop, calls=%fused_computation.16 | loop fusion | flops 4928000 | bytes 7168012 | tf_op jit(solution)/shard_map/convert_element_type | solution.py:196
  (319 shorter events, 188.3 us)
Async XLA Ops:
  7.2 366.3 %reduce-scatter.2.cloned.1.call-start = ((), (), s32[]{:S(2)}) async-start(), calls=%async_computation.1 | async-start | bytes 15597568 | tf_op jit(solution)/shard_map/reduce_scatter | solution.py:197
  9.6 13.4 %collective-permute-start.48 = (bf16[64,1000]{1,0:T(8,128)(2,1)}, bf16[64,1000]{1,0:T(8,128)(2,1)S(1)}, u32[]{:S(2)}, u32[]{:S(2)}) collective-permute-start(bf16[64,1000]{1,0:T(8,128)(2,1)} %dynamic-slice_bitcast_fusion.16), channel_id=1, source_target_pairs={{0,16},{16,0},{32,48},{48,32},{64,80},{80,64},{96,112},{112,96},{1... | collective-permute-start | bytes 384008 | tf_op jit(solution)/shard_map/ppermute | solution.py:48
  13.3 12.9 %collective-permute-start = (bf16[64,1000]{1,0:T(8,128)(2,1)}, bf16[64,1000]{1,0:T(8,128)(2,1)}, u32[]{:S(2)}, u32[]{:S(2)}) collective-permute-start(bf16[64,1000]{1,0:T(8,128)(2,1)} %get-tuple-element.41), channel_id=1, source_target_pairs={{0,1},{1,2},{2,3},{3,0},{4,5},{5,6},{6,7},{7,4},{8,9},{9,10},{10,1... | collective-permute-start | bytes 384008 | tf_op jit(solution)/shard_map/ppermute | solution.py:48
  14.6 12.4 %collective-permute-start.2 = (bf16[64,1000]{1,0:T(8,128)(2,1)}, bf16[64,1000]{1,0:T(8,128)(2,1)}, u32[]{:S(2)}, u32[]{:S(2)}) collective-permute-start(bf16[64,1000]{1,0:T(8,128)(2,1)} %get-tuple-element.42), channel_id=1, source_target_pairs={{0,3},{1,0},{2,1},{3,2},{4,7},{5,4},{6,5},{7,6},{8,11},{9,8},{10,9... | collective-permute-start | bytes 384008 | tf_op jit(solution)/shard_map/ppermute | solution.py:48
  16.0 11.0 %collective-permute-start.1 = (bf16[64,1000]{1,0:T(8,128)(2,1)}, bf16[64,1000]{1,0:T(8,128)(2,1)}, u32[]{:S(2)}, u32[]{:S(2)}) collective-permute-start(bf16[64,1000]{1,0:T(8,128)(2,1)} %get-tuple-element.43), channel_id=1, source_target_pairs={{0,2},{1,3},{2,0},{3,1},{4,6},{5,7},{6,4},{7,5},{8,10},{9,11},{10,... | collective-permute-start | bytes 384008 | tf_op jit(solution)/shard_map/ppermute | solution.py:48
  45.3 10.5 %collective-permute-start.53 = (bf16[64,1000]{1,0:T(8,128)(2,1)}, bf16[64,1000]{1,0:T(8,128)(2,1)S(1)}, u32[]{:S(2)}, u32[]{:S(2)}) collective-permute-start(bf16[64,1000]{1,0:T(8,128)(2,1)} %get-tuple-element.29), channel_id=1, source_target_pairs={{0,1},{1,2},{2,3},{3,0},{4,5},{5,6},{6,7},{7,4},{8,9},{9,10},{10,1... | collective-permute-start | bytes 384008 | tf_op jit(solution)/shard_map/ppermute | solution.py:48
  45.3 10.5 %collective-permute-start.55 = (bf16[64,1000]{1,0:T(8,128)(2,1)}, bf16[64,1000]{1,0:T(8,128)(2,1)}, u32[]{:S(2)}, u32[]{:S(2)}) collective-permute-start(bf16[64,1000]{1,0:T(8,128)(2,1)} %get-tuple-element.30), channel_id=1, source_target_pairs={{0,3},{1,0},{2,1},{3,2},{4,7},{5,4},{6,5},{7,6},{8,11},{9,8},{10,9... | collective-permute-start | bytes 384008 | tf_op jit(solution)/shard_map/ppermute | solution.py:48
  58.5 11.7 %collective-permute-start.12 = (bf16[64,1000]{1,0:T(8,128)(2,1)S(1)}, bf16[64,1000]{1,0:T(8,128)(2,1)S(1)}, u32[]{:S(2)}, u32[]{:S(2)}) collective-permute-start(bf16[64,1000]{1,0:T(8,128)(2,1)S(1)} %fusion.142), channel_id=1, source_target_pairs={{0,96},{16,112},{32,0},{48,16},{64,32},{80,48},{96,64},{112,80},{1... | collective-permute-start | bytes 384008 | tf_op jit(solution)/shard_map/ppermute | solution.py:37
  61.3 10.9 %collective-permute-start.11 = (bf16[64,1000]{1,0:T(8,128)(2,1)S(1)}, bf16[64,1000]{1,0:T(8,128)(2,1)S(1)}, u32[]{:S(2)}, u32[]{:S(2)}) collective-permute-start(bf16[64,1000]{1,0:T(8,128)(2,1)S(1)} %fusion.142), channel_id=1, source_target_pairs={{0,64},{16,80},{32,96},{48,112},{64,0},{80,16},{96,32},{112,48},{1... | collective-permute-start | bytes 384008 | tf_op jit(solution)/shard_map/ppermute | solution.py:37
  62.2 10.0 %collective-permute-start.10 = (bf16[64,1000]{1,0:T(8,128)(2,1)S(1)}, bf16[64,1000]{1,0:T(8,128)(2,1)S(1)}, u32[]{:S(2)}, u32[]{:S(2)}) collective-permute-start(bf16[64,1000]{1,0:T(8,128)(2,1)S(1)} %fusion.142), channel_id=1, source_target_pairs={{0,32},{16,48},{32,64},{48,80},{64,96},{80,112},{96,0},{112,16},{1... | collective-permute-start | bytes 384008 | tf_op jit(solution)/shard_map/ppermute | solution.py:37
  64.4 9.3 %collective-permute-start.61 = (bf16[64,1000]{1,0:T(8,128)(2,1)S(1)}, bf16[64,1000]{1,0:T(8,128)(2,1)S(1)}, u32[]{:S(2)}, u32[]{:S(2)}) collective-permute-start(bf16[64,1000]{1,0:T(8,128)(2,1)S(1)} %add_convert_fusion.5), channel_id=1, source_target_pairs={{0,1},{1,2},{2,3},{3,0},{4,5},{5,6},{6,7},{7,4},{8,9},{9,10},{10,1... | collective-permute-start | bytes 384008 | tf_op jit(solution)/shard_map/ppermute | solution.py:57
  66.4 9.5 %collective-permute-start.60 = (bf16[64,1000]{1,0:T(8,128)(2,1)S(1)}, bf16[64,1000]{1,0:T(8,128)(2,1)S(1)}, u32[]{:S(2)}, u32[]{:S(2)}) collective-permute-start(bf16[64,1000]{1,0:T(8,128)(2,1)S(1)} %add_convert_fusion.5), channel_id=1, source_target_pairs={{0,2},{1,3},{2,0},{3,1},{4,6},{5,7},{6,4},{7,5},{8,10},{9,11},{10,... | collective-permute-start | bytes 384008 | tf_op jit(solution)/shard_map/ppermute | solution.py:57
  116.7 15.6 %collective-permute-start.72 = (bf16[64,1000]{1,0:T(8,128)(2,1)S(1)}, bf16[64,1000]{1,0:T(8,128)(2,1)S(1)}, u32[]{:S(2)}, u32[]{:S(2)}) collective-permute-start(bf16[64,1000]{1,0:T(8,128)(2,1)S(1)} %fusion.125), channel_id=1, source_target_pairs={{0,12},{1,13},{2,14},{3,15},{4,0},{5,1},{6,2},{7,3},{8,4},{9,5},{1... | collective-permute-start | bytes 384008 | tf_op jit(solution)/shard_map/ppermute | solution.py:37
  137.7 12.7 %collective-permute-start.26 = (bf16[64,1000]{1,0:T(8,128)(2,1)S(1)}, bf16[64,1000]{1,0:T(8,128)(2,1)S(1)}, u32[]{:S(2)}, u32[]{:S(2)}) collective-permute-start(bf16[64,1000]{1,0:T(8,128)(2,1)S(1)} %fusion.138), channel_id=1, source_target_pairs={{0,96},{16,112},{32,0},{48,16},{64,32},{80,48},{96,64},{112,80},{1... | collective-permute-start | bytes 384008 | tf_op jit(solution)/shard_map/ppermute | solution.py:37
  139.5 10.9 %collective-permute-start.25 = (bf16[64,1000]{1,0:T(8,128)(2,1)S(1)}, bf16[64,1000]{1,0:T(8,128)(2,1)S(1)}, u32[]{:S(2)}, u32[]{:S(2)}) collective-permute-start(bf16[64,1000]{1,0:T(8,128)(2,1)S(1)} %fusion.138), channel_id=1, source_target_pairs={{0,64},{16,80},{32,96},{48,112},{64,0},{80,16},{96,32},{112,48},{1... | collective-permute-start | bytes 384008 | tf_op jit(solution)/shard_map/ppermute | solution.py:37
  141.1 9.9 %collective-permute-start.24 = (bf16[64,1000]{1,0:T(8,128)(2,1)S(1)}, bf16[64,1000]{1,0:T(8,128)(2,1)}, u32[]{:S(2)}, u32[]{:S(2)}) collective-permute-start(bf16[64,1000]{1,0:T(8,128)(2,1)S(1)} %fusion.138), channel_id=1, source_target_pairs={{0,32},{16,48},{32,64},{48,80},{64,96},{80,112},{96,0},{112,16},{1... | collective-permute-start | bytes 384008 | tf_op jit(solution)/shard_map/ppermute | solution.py:37
  143.3 11.3 %collective-permute-start.76 = (bf16[64,1000]{1,0:T(8,128)(2,1)S(1)}, bf16[64,1000]{1,0:T(8,128)(2,1)S(1)}, u32[]{:S(2)}, u32[]{:S(2)}) collective-permute-start(bf16[64,1000]{1,0:T(8,128)(2,1)S(1)} %dynamic-slice_bitcast_fusion.8), channel_id=1, source_target_pairs={{0,16},{16,0},{32,48},{48,32},{64,80},{80,64},{96,112},{112,96},{1... | collective-permute-start | bytes 384008 | tf_op jit(solution)/shard_map/ppermute | solution.py:48
  183.8 9.3 %collective-permute-start.84 = (bf16[64,1000]{1,0:T(8,128)(2,1)S(1)}, bf16[64,1000]{1,0:T(8,128)(2,1)S(1)}, u32[]{:S(2)}, u32[]{:S(2)}) collective-permute-start(bf16[64,1000]{1,0:T(8,128)(2,1)S(1)} %fusion.121), channel_id=1, source_target_pairs={{0,4},{1,5},{2,6},{3,7},{4,8},{5,9},{6,10},{7,11},{8,12},{9,13},{1... | collective-permute-start | bytes 384008 | tf_op jit(solution)/shard_map/ppermute | solution.py:37
  185.3 11.5 %collective-permute-start.36 = (bf16[64,1000]{1,0:T(8,128)(2,1)S(1)}, bf16[64,1000]{1,0:T(8,128)(2,1)S(1)}, u32[]{:S(2)}, u32[]{:S(2)}) collective-permute-start(bf16[64,1000]{1,0:T(8,128)(2,1)S(1)} %add_convert_fusion.9), channel_id=1, source_target_pairs={{0,1},{1,2},{2,3},{3,0},{4,5},{5,6},{6,7},{7,4},{8,9},{9,10},{10,1... | collective-permute-start | bytes 384008 | tf_op jit(solution)/shard_map/ppermute | solution.py:57
  212.8 9.7 %collective-permute-start.91 = (bf16[64,1000]{1,0:T(8,128)(2,1)S(1)}, bf16[64,1000]{1,0:T(8,128)(2,1)S(1)}, u32[]{:S(2)}, u32[]{:S(2)}) collective-permute-start(bf16[64,1000]{1,0:T(8,128)(2,1)S(1)} %fusion.118), channel_id=1, source_target_pairs={{0,32},{16,48},{32,64},{48,80},{64,96},{80,112},{96,0},{112,16},{1... | collective-permute-start | bytes 384008 | tf_op jit(solution)/shard_map/ppermute | solution.py:37
  244.8 9.7 %collective-permute-start.38 = (bf16[64,1000]{1,0:T(8,128)(2,1)S(1)}, bf16[64,1000]{1,0:T(8,128)(2,1)S(1)}, u32[]{:S(2)}, u32[]{:S(2)}) collective-permute-start(bf16[64,1000]{1,0:T(8,128)(2,1)S(1)} %fusion.134), channel_id=1, source_target_pairs={{0,32},{16,48},{32,64},{48,80},{64,96},{80,112},{96,0},{112,16},{1... | collective-permute-start | bytes 384008 | tf_op jit(solution)/shard_map/ppermute | solution.py:37
  257.8 9.8 %collective-permute-start.42 = (bf16[64,1000]{1,0:T(8,128)(2,1)S(1)}, bf16[64,1000]{1,0:T(8,128)(2,1)S(1)}, u32[]{:S(2)}, u32[]{:S(2)}) collective-permute-start(bf16[64,1000]{1,0:T(8,128)(2,1)S(1)} %get-tuple-element.32), channel_id=1, source_target_pairs={{0,1},{1,2},{2,3},{3,0},{4,5},{5,6},{6,7},{7,4},{8,9},{9,10},{10,1... | collective-permute-start | bytes 384008 | tf_op jit(solution)/shard_map/ppermute | solution.py:48
  257.9 9.7 %collective-permute-start.44 = (bf16[64,1000]{1,0:T(8,128)(2,1)S(1)}, bf16[64,1000]{1,0:T(8,128)(2,1)S(1)}, u32[]{:S(2)}, u32[]{:S(2)}) collective-permute-start(bf16[64,1000]{1,0:T(8,128)(2,1)S(1)} %get-tuple-element.33), channel_id=1, source_target_pairs={{0,3},{1,0},{2,1},{3,2},{4,7},{5,4},{6,5},{7,6},{8,11},{9,8},{10,9... | collective-permute-start | bytes 384008 | tf_op jit(solution)/shard_map/ppermute | solution.py:48
  260.6 12.0 %collective-permute-start.43 = (bf16[64,1000]{1,0:T(8,128)(2,1)S(1)}, bf16[64,1000]{1,0:T(8,128)(2,1)S(1)}, u32[]{:S(2)}, u32[]{:S(2)}) collective-permute-start(bf16[64,1000]{1,0:T(8,128)(2,1)S(1)} %get-tuple-element.34), channel_id=1, source_target_pairs={{0,2},{1,3},{2,0},{3,1},{4,6},{5,7},{6,4},{7,5},{8,10},{9,11},{10,... | collective-permute-start | bytes 384008 | tf_op jit(solution)/shard_map/ppermute | solution.py:48
  272.9 12.7 %collective-permute-start.45 = (bf16[64,1000]{1,0:T(8,128)(2,1)S(1)}, bf16[64,1000]{1,0:T(8,128)(2,1)}, u32[]{:S(2)}, u32[]{:S(2)}) collective-permute-start(bf16[64,1000]{1,0:T(8,128)(2,1)S(1)} %fusion.133), channel_id=1, source_target_pairs={{0,4},{1,5},{2,6},{3,7},{4,8},{5,9},{6,10},{7,11},{8,12},{9,13},{1... | collective-permute-start | bytes 384008 | tf_op jit(solution)/shard_map/ppermute | solution.py:37
  286.6 12.8 %collective-permute-start.97 = (bf16[64,1000]{1,0:T(8,128)(2,1)S(1)}, bf16[64,1000]{1,0:T(8,128)(2,1)S(1)}, u32[]{:S(2)}, u32[]{:S(2)}) collective-permute-start(bf16[64,1000]{1,0:T(8,128)(2,1)S(1)} %add_convert_fusion.7), channel_id=1, source_target_pairs={{0,1},{1,2},{2,3},{3,0},{4,5},{5,6},{6,7},{7,4},{8,9},{9,10},{10,1... | collective-permute-start | bytes 384008 | tf_op jit(solution)/shard_map/ppermute | solution.py:57
  287.9 12.6 %collective-permute-start.96 = (bf16[64,1000]{1,0:T(8,128)(2,1)S(1)}, bf16[64,1000]{1,0:T(8,128)(2,1)S(1)}, u32[]{:S(2)}, u32[]{:S(2)}) collective-permute-start(bf16[64,1000]{1,0:T(8,128)(2,1)S(1)} %add_convert_fusion.7), channel_id=1, source_target_pairs={{0,2},{1,3},{2,0},{3,1},{4,6},{5,7},{6,4},{7,5},{8,10},{9,11},{10,... | collective-permute-start | bytes 384008 | tf_op jit(solution)/shard_map/ppermute | solution.py:57
  289.0 12.5 %collective-permute-start.95 = (bf16[64,1000]{1,0:T(8,128)(2,1)S(1)}, bf16[64,1000]{1,0:T(8,128)(2,1)S(1)}, u32[]{:S(2)}, u32[]{:S(2)}) collective-permute-start(bf16[64,1000]{1,0:T(8,128)(2,1)S(1)} %add_convert_fusion.7), channel_id=1, source_target_pairs={{0,3},{1,0},{2,1},{3,2},{4,7},{5,4},{6,5},{7,6},{8,11},{9,8},{10,9... | collective-permute-start | bytes 384008 | tf_op jit(solution)/shard_map/ppermute | solution.py:57
  310.4 9.3 %collective-permute-start.98 = (bf16[4,448,1000]{2,1,0:T(8,128)(2,1)}, bf16[4,448,1000]{2,1,0:T(8,128)(2,1)}, u32[]{:S(2)}, u32[]{:S(2)}) collective-permute-start(bf16[4,448,1000]{2,1,0:T(8,128)(2,1)} %dynamic-slice_bitcast_fusion), channel_id=1, source_target_pairs={{0,16},{16,0},{32,48},{48,32},{64,80},{80,64},{96,112},{112,96},{1... | collective-permute-start | bytes 10752008 | tf_op jit(solution)/shard_map/ppermute | solution.py:72
  326.6 42.8 %collective-permute-start.99 = (bf16[448,1000]{1,0:T(8,128)(2,1)}, bf16[448,1000]{1,0:T(8,128)(2,1)}, u32[]{:S(2)}, u32[]{:S(2)}) collective-permute-start(bf16[448,1000]{1,0:T(8,128)(2,1)} %get-tuple-element.14), channel_id=1, source_target_pairs={{0,32},{16,48},{32,64},{48,80},{64,96},{80,112},{96,0},{112,16},{1... | collective-permute-start | bytes 2688008 | tf_op jit(solution)/shard_map/ppermute | solution.py:81
  326.6 42.8 %collective-permute-start.101 = (bf16[448,1000]{1,0:T(8,128)(2,1)}, bf16[448,1000]{1,0:T(8,128)(2,1)}, u32[]{:S(2)}, u32[]{:S(2)}) collective-permute-start(bf16[448,1000]{1,0:T(8,128)(2,1)} %get-tuple-element.15), channel_id=1, source_target_pairs={{0,96},{16,112},{32,0},{48,16},{64,32},{80,48},{96,64},{112,80},{1... | collective-permute-start | bytes 2688008 | tf_op jit(solution)/shard_map/ppermute | solution.py:81
  329.2 40.1 %collective-permute-start.100 = (bf16[448,1000]{1,0:T(8,128)(2,1)}, bf16[448,1000]{1,0:T(8,128)(2,1)}, u32[]{:S(2)}, u32[]{:S(2)}) collective-permute-start(bf16[448,1000]{1,0:T(8,128)(2,1)} %get-tuple-element.16), channel_id=1, source_target_pairs={{0,64},{16,80},{32,96},{48,112},{64,0},{80,16},{96,32},{112,48},{1... | collective-permute-start | bytes 2688008 | tf_op jit(solution)/shard_map/ppermute | solution.py:81
  (85 other events, 770.2 us)
Sparse Core Ops, SparseCore 0:
  240.4 111.7 reduce-scatter.1
